TPU v7x, 256 devices: a whole 4x4x8 slice. The times are simulated.
256 devices in a mesh: tile: 64 (over y_hi, z, x), fsdp: 4 (over y_lo, core).
Axes of the slice: x: 4, y: 4 (y_hi: 2, y_lo: 2; y = y_hi * 2 + y_lo), z: 8, core: 2. Of those that a mesh axis runs over, the one named last changes fastest.
Arguments:
- fields: bfloat16 [4, 32, 512, 512], P('fsdp', None, 'tile'), may hold values from -6 to 6
- seam_shift: int32 [64, 2], P('tile'), may hold values from -4 to 4
- kernel: float32 [49, 512], replicated, may hold values from -0.875 to 0.875
- gain: float32 [512], replicated, may hold values from 0.3 to 3
- w_in: bfloat16 [512, 2048], P(None, 'fsdp'), may hold values from -0.25 to 0.25
- w_out: bfloat16 [2048, 512], P('fsdp'), may hold values from -0.125 to 0.125
- cotangent: bfloat16 [4, 32, 512, 512], P('fsdp', None, 'tile'), may hold values from -6 to 6
Outputs:
- mixed: bfloat16 [4, 32, 512, 512], P('fsdp', None, 'tile')
- field_grad: bfloat16 [4, 32, 512, 512], P('fsdp', None, 'tile')
- kernel_grad: float32 [49, 512], replicated
- gain_grad: float32 [512], replicated
- w_in_grad: float32 [512, 2048], P(None, 'fsdp')
- w_out_grad: float32 [2048, 512], P('fsdp')
Inputs may be any that keep to these rules, and one draw needn't show every extreme that they name: `seam_shift`: offset added to the row index of cells taken across a tile's west (column 0) or east (column 1) seam.
All inputs are finite; a program needn't handle non-finite values.
Results may differ from a plain program's by a relative error of at most 0.0095.
Values may be sent and summed in bfloat16 or wider, within the bound.
No kernel may reach another device: no remote copies, remote signals or barrier semaphores. Data moves between devices by JAX's collectives and lax.ppermute only.
A program may use at most 128 MiB of HBM per device.

v0:
```python
import math

import jax
import jax.numpy as jnp
from jax import lax
from jax.sharding import PartitionSpec as P

eps = 1e-06
inv_root2 = 0.7071067811865476
inv_root_tau = 0.3989422804014327


def extended(cells, sides, width):
    for axis, dim in sides:
        count = lax.axis_size(axis)
        head = lax.slice_in_dim(cells, 0, width, axis=dim)
        tail = lax.slice_in_dim(cells, cells.shape[dim] - width, cells.shape[dim], axis=dim)
        cells = jnp.concatenate(
            [
                lax.ppermute(tail, axis, [(i, (i + 1) % count) for i in range(count)]),
                cells,
                lax.ppermute(head, axis, [((i + 1) % count, i) for i in range(count)]),
            ],
            axis=dim,
        )
    return cells


def exchange(value, axis, bit):
    count = lax.axis_size(axis)
    return lax.ppermute(value, axis, [(i, i ^ (1 << bit)) for i in range(count)])


def fsdp_summed(stacked):
    me = lax.axis_index("fsdp")
    for bit in (0, 1):
        half = stacked.shape[0] // 2
        side = (me >> bit) & 1
        keep = lax.dynamic_slice_in_dim(stacked, side * half, half, 0).astype(jnp.bfloat16)
        send = lax.dynamic_slice_in_dim(stacked, (1 - side) * half, half, 0).astype(jnp.bfloat16)
        got = exchange(send, "fsdp", bit)
        stacked = keep.astype(jnp.float32) + got.astype(jnp.float32)
    return stacked


def tile_summed(chunk):
    assert lax.axis_size("tile") == 64
    me = lax.axis_index("tile")
    groups = ((0, 1), (2, 3), (4, 5))

    def masks(group):
        mine = ((me >> group[0]) & 1) * 2 + ((me >> group[1]) & 1)
        return mine, [(d, ((d >> 1) << group[0]) | ((d & 1) << group[1])) for d in (1, 2, 3)]

    for group in groups[:-1]:
        mine, partners = masks(group)
        size = chunk.shape[0] // 4
        total = lax.dynamic_slice_in_dim(chunk, mine * size, size, 0)
        for d, mask in partners:
            send = lax.dynamic_slice_in_dim(chunk, (mine ^ d) * size, size, 0)
            total = total + swapped(send.astype(jnp.bfloat16), "tile", mask).astype(jnp.float32)
        chunk = total
    mine, partners = masks(groups[-1])
    own = chunk.astype(jnp.bfloat16)
    blocks = jnp.stack([own] + [swapped(own, "tile", mask) for _, mask in partners])
    total = None
    for place in range(4):
        block = lax.dynamic_index_in_dim(blocks, place ^ mine, 0, keepdims=False).astype(jnp.float32)
        total = block if total is None else total + block
    chunk = total.astype(jnp.bfloat16)
    for group in reversed(groups[:-1]):
        mine, partners = masks(group)
        size = chunk.shape[0]
        whole = jnp.zeros((4 * size,) + chunk.shape[1:], chunk.dtype)
        whole = lax.dynamic_update_slice_in_dim(whole, chunk, mine * size, 0)
        for d, mask in partners:
            got = swapped(chunk, "tile", mask)
            whole = lax.dynamic_update_slice_in_dim(whole, got, (mine ^ d) * size, 0)
        chunk = whole
    return chunk.astype(jnp.float32)


def swapped(value, axis, mask):
    count = lax.axis_size(axis)
    return lax.ppermute(value, axis, [(i, i ^ mask) for i in range(count)])


def gathered(shard, anchor):
    me = lax.axis_index("fsdp")
    high, low = (me >> 1) & 1, me & 1
    got = exchange(shard, "fsdp", 1)
    pair = jnp.stack([jnp.where(high == 0, shard, got), jnp.where(high == 0, got, shard)])
    pair, anchor = lax.optimization_barrier((pair, anchor))
    other = exchange(pair, "fsdp", 0)
    first, second = jnp.where(low == 0, pair, other), jnp.where(low == 0, other, pair)
    return jnp.stack([first, second], axis=1).reshape((4,) + shard.shape), anchor


def gelu(value):
    return value * 0.5 * (1.0 + lax.erf(value * inv_root2))


def gelu_slope(value):
    return 0.5 * (1.0 + lax.erf(value * inv_root2)) + value * inv_root_tau * jnp.exp(
        -0.5 * value * value
    )


def shift_rows(strip, offset):
    height = strip.shape[1]
    wider = jnp.pad(strip, ((0, 0), (height, height), (0, 0), (0, 0)))
    return lax.dynamic_slice_in_dim(wider, height + offset, height, 1)


def depthwise(padded, kernel):
    height = padded.shape[1] - 6
    width = padded.shape[2] - 6
    total = jnp.zeros((padded.shape[0], height, width, padded.shape[3]), jnp.float32)
    for row in range(7):
        for col in range(7):
            total = (
                total + padded[:, row : row + height, col : col + width, :] * kernel[7 * row + col]
            )
    return total


def body(fields, seam_shift, kernel, gain, w_in, w_out, cotangent):
    height = fields.shape[1]
    width = fields.shape[2]
    channels = fields.shape[3]
    count = fields.shape[0] * height * width
    cells = count * lax.axis_size("tile") * lax.axis_size("fsdp")
    factor = 1.0 / math.sqrt(cells)
    west_shift = seam_shift[0, 0]
    east_shift = seam_shift[0, 1]
    row_pad = ((0, 0), (3, 3), (0, 0), (0, 0))
    widened = extended(fields, (("tile", 2),), 3)
    west = shift_rows(widened[:, :, :3], west_shift)
    east = shift_rows(widened[:, :, width + 3 :], east_shift)
    padded = jnp.pad(jnp.concatenate([west, fields, east], axis=2), row_pad)
    mixed_in = depthwise(padded, kernel)
    rows = mixed_in.reshape(count, channels)
    mean = jnp.mean(rows, axis=-1, keepdims=True)
    centered = rows - mean
    rstd = lax.rsqrt(jnp.mean(centered * centered, axis=-1, keepdims=True) + eps)
    normed = centered * rstd
    scaled = (normed * gain).astype(jnp.bfloat16)
    back = cotangent.reshape(count, channels)
    contract_last = (((1,), (1,)), ((), ()))
    both, scaled = gathered(jnp.stack([w_in, w_out]), scaled)
    full_in = jnp.concatenate([both[f, 0] for f in range(both.shape[0])], axis=1)
    full_out = both[:, 1].reshape(-1, w_out.shape[1])
    pre = jnp.dot(scaled, full_in, preferred_element_type=jnp.float32)
    hidden = gelu(pre).astype(jnp.bfloat16)
    branch = jnp.dot(hidden, full_out, preferred_element_type=jnp.float32)
    d_hidden = lax.dot_general(back, full_out, contract_last, preferred_element_type=jnp.float32)
    residual = fields.reshape(count, channels).astype(jnp.float32)
    mixed = (residual + branch).astype(jnp.bfloat16).reshape(fields.shape)
    d_pre = (d_hidden * gelu_slope(pre)).astype(jnp.bfloat16)
    d_scaled = lax.dot_general(d_pre, full_in, contract_last, preferred_element_type=jnp.float32)
    term_gain = jnp.sum(d_scaled * normed, axis=0) * factor
    d_normed = d_scaled * gain
    d_rows = (
        d_normed
        - jnp.mean(d_normed, axis=-1, keepdims=True)
        - normed * jnp.mean(d_normed * normed, axis=-1, keepdims=True)
    ) * rstd
    d_mixed = d_rows.reshape(mixed_in.shape)
    unused, pullback = jax.vjp(depthwise, padded.astype(jnp.float32), kernel)
    d_padded, kernel_term = pullback(d_mixed)
    kernel_term = kernel_term * factor
    d_core = d_padded[:, 3 : height + 3]
    d_west = shift_rows(d_core[:, :, :3], -west_shift)
    d_east = shift_rows(d_core[:, :, width + 3 :], -east_shift)
    returned = extended(
        jnp.concatenate([d_west, d_east], axis=2).astype(jnp.bfloat16), (("tile", 2),), 3
    ).astype(jnp.float32)
    own = cotangent.astype(jnp.float32) + d_core[:, :, 3 : width + 3]
    field_grad = jnp.concatenate(
        [
            own[:, :, :3] + returned[:, :, :3],
            own[:, :, 3 : width - 3],
            own[:, :, width - 3 :] + returned[:, :, 9:],
        ],
        axis=2,
    ).astype(jnp.bfloat16)
    parts = lax.axis_size("fsdp")
    assert parts == 4
    share = full_in.shape[1] // parts
    owners = [0, 2, 1, 3]
    contract_rows = (((0,), (0,)), ((), ()))
    term_in4 = jnp.stack(
        [
            lax.dot_general(
                scaled, d_pre[:, f * share : (f + 1) * share], contract_rows,
                preferred_element_type=jnp.float32,
            )
            for f in owners
        ]
    ).reshape(2, 2, channels, share)
    term_out4 = jnp.stack(
        [
            lax.dot_general(
                hidden[:, f * share : (f + 1) * share], back, contract_rows,
                preferred_element_type=jnp.float32,
            )
            for f in owners
        ]
    ).reshape(2, 2, share, channels)
    spare = -(kernel_term.shape[0] + 1) % 64
    small = jnp.concatenate(
        [kernel_term, term_gain[None], jnp.zeros((spare, channels), jnp.float32)], axis=0
    )
    small4 = jnp.broadcast_to(small, (2, 2) + small.shape)
    stacked = jnp.concatenate(
        [
            (term_in4 * factor).astype(jnp.bfloat16),
            small4.astype(jnp.bfloat16),
            (term_out4 * factor).astype(jnp.bfloat16),
        ],
        axis=2,
    ).reshape(-1, channels)
    chunk = fsdp_summed(stacked)
    first = channels + small.shape[0]
    total = tile_summed(chunk)
    low, high = total[:first], total[first:]
    w_in_grad = low[:channels]
    kernel_grad = low[channels : channels + kernel_term.shape[0]]
    gain_grad = low[channels + kernel_term.shape[0]]
    w_out_grad = high
    return (mixed, field_grad, kernel_grad, gain_grad, w_in_grad, w_out_grad)


def solution(mesh):
    return jax.shard_map(
        body,
        mesh=mesh,
        in_specs=(
            P("fsdp", None, "tile", None),
            P("tile", None),
            P(),
            P(),
            P(None, "fsdp"),
            P("fsdp", None),
            P("fsdp", None, "tile", None),
        ),
        out_specs=(
            P("fsdp", None, "tile", None),
            P("fsdp", None, "tile", None),
            P(),
            P(),
            P(None, "fsdp"),
            P("fsdp", None),
        ),
        check_vma=False,
    )
```

profile of v0, /device:TPU:32, one launch (start us, length us, event | category | flops | bytes accessed | tf_op | source)
XLA Modules:
  0.0 166.7 jit_solution(3571895005758621886)
XLA Ops:
  0.7 1.2 fusion.122
  1.8 1.6 collective-permute-start.1
  3.4 2.6 %collective-permute-start.2 = (bf16[1,32,3,512]{3,2,1,0:T(4,128)(2,1)S(1)}, bf16[1,32,3,512]{3,2,1,0:T(4,128)(2,1)S(1)}, u32[]{:S(2)}, u32[]{:S(2)}) collective-permute-start(bf16[1,32,3,512]{3,2,1,0:T(4,128)(2,1)S(1)} %get-tuple-element.137), channel_id=1, source_target_pairs={{4,0},{8,4},{12,8},{16,12},{20,16},{24,20},{28,24},{32,28},{36,32}... | collective-permute-start | bytes 294920 | tf_op jit(solution)/shard_map/ppermute | solution.py:22
  6.1 2.3 %pad_maximum_fusion.4 = bf16[2,512,512]{2,1,0:T(8,128)(2,1)} fusion(bf16[1,512,512]{2,1,0:T(8,128)(2,1)} %bitcast.314, bf16[1,512,512]{2,1,0:T(8,128)(2,1)} %bitcast.316), kind=kLoop, calls=%fused_computation.38 | loop fusion | flops 524288 | bytes 2097152 | tf_op jit(solution)/shard_map/stack | solution.py:150
  8.3 1.6 collective-permute-start
  10.0 0.6 fusion.126
  13.8 4.4 %fusion.118 = (f32[32,8]{1,0:T(8,128)S(1)}, f32[1,32,8,512]{3,2,1,0:T(8,128)S(1)}) fusion(f32[512]{0:T(512)S(1)} %bitcast.340, bf16[1,38,14,512]{3,2,1,0:T(8,128)(2,1)S(1)} %get-tuple-element.64, f32[512]{0:T(512)S(1)} %bitcast.358, f32[512]{0:T(512)S(1)} %bitcast.394, f32[512]{0:T(512)S(1)} %bitcast.396, f32[512]{0:T(512)S(1)} %bitcast.398, ...), kind=kLoop, calls=%fused_computation.303 | loop fusion | flops 21626624 | bytes 12094464 | tf_op jit(solution)/shard_map/reduce_sum | solution.py:143
  18.8 14.2 %collective-permute-done = bf16[2,512,512]{2,1,0:T(8,128)(2,1)} collective-permute-done((bf16[2,512,512]{2,1,0:T(8,128)(2,1)}, bf16[2,512,512]{2,1,0:T(8,128)(2,1)}, u32[]{:S(2)}, u32[]{:S(2)}) %collective-permute-start) | collective-permute-done | bytes 1048608 | tf_op jit(solution)/shard_map/ppermute | solution.py:31
  33.0 1.5 select_bitcast_fusion.3
  34.5 1.5 pad_maximum_fusion.2
  36.1 4.4 %collective-permute-done.3 = bf16[2,2,512,512]{3,2,1,0:T(8,128)(2,1)} collective-permute-done((bf16[2,2,512,512]{3,2,1,0:T(8,128)(2,1)}, bf16[2,2,512,512]{3,2,1,0:T(8,128)(2,1)}, u32[]{:S(2)}, u32[]{:S(2)}) %collective-permute-start.3) | collective-permute-done | bytes 2097184 | tf_op jit(solution)/shard_map/ppermute | solution.py:31
  40.5 2.5 %select_bitcast_fusion.1 = (bf16[2,1,2,512,512]{4,3,2,1,0:T(8,128)(2,1)S(1)}, bf16[2,1,2,512,512]{4,3,2,1,0:T(8,128)(2,1)S(1)}) fusion(bf16[2,2,512,512]{3,2,1,0:T(8,128)(2,1)} %pad_maximum_fusion.2, bf16[2,2,512,512]{3,2,1,0:T(8,128)(2,1)} %collective-permute-done.3, pred[]{:T(512)S(6)} %eq.9), kind=kLoop, calls=%fused_computation.22 | loop fusion | flops 2097152 | bytes 8388609 | tf_op jit(solution)/shard_map/stack | solution.py:96
  43.0 0.4 pad_maximum_fusion.1
  43.8 0.8 multiply_convert_fusion
  44.6 0.4 copy-done.3
  44.9 1.3 fusion.3
  46.2 0.9 multiply_reduce_fusion
  47.1 2.1 %fusion.86 = (f32[512]{0:T(512)S(1)}, f32[512]{0:T(512)S(1)}, f32[512]{0:T(512)S(1)}, f32[512]{0:T(512)S(1)}, f32[512]{0:T(512)S(1)}, /*index=5*/f32[512]{0:T(51...) fusion(f32[1,38,14,512]{3,2,1,0:T(8,128)S(1)} %get-tuple-elemen, ...), kind=kLoop, calls=%fused_computation.180 | loop fusion | flops 4318720 | bytes 8421376 | tf_op jit(solution)/shard_map/transpose(jvp())/reduce_sum | solution.py:122
  49.3 0.9 fusion.87
  50.2 1.0 fusion.88
  54.2 0.6 fusion
  54.7 0.6 fusion.1
  55.4 0.3 pad_maximum_fusion
  55.7 1.7 %constant_dynamic-slice_fusion = bf16[2176,512]{1,0:T(8,128)(2,1)} fusion(bf16[4352,512]{1,0:T(8,128)(2,1)S(1)} %bitcast.304, s32[]{:T(128)S(6)} %select_n.104), kind=kLoop, calls=%fused_computation.296 | loop fusion | bytes 4456452 | tf_op jit(solution)/shard_map/dynamic_slice | solution.py:40
  57.4 1.1 copy-done
  60.0 0.9 bitcast_multiply_fusion.46
  60.8 1.3 bitcast_multiply_fusion.47
  62.1 1.3 bitcast_multiply_fusion.48
  63.4 2.3 %convert_add_fusion = bf16[2176,512]{1,0:T(8,128)(2,1)S(1)} fusion(bf16[2176,512]{1,0:T(8,128)(2,1)} %collective-permute-done.6, bf16[4352,512]{1,0:T(8,128)(2,1)S(1)} %bitcast.307, s32[]{:T(128)S(6)} %select_n.103), kind=kLoop, calls=%fused_computation.1 | loop fusion | flops 4456448 | bytes 6684676 | tf_op jit(solution)/shard_map/add | solution.py:42
  65.8 1.7 collective-permute-start.7
  67.4 6.7 %pad_add_fusion = f32[1,38,14,512]{3,2,1,0:T(8,128)S(1)} fusion(f32[1,32,8,512]{3,2,1,0:T(8,128)S(1)} %get-tuple-element.88, f32[1,32,8,512]{3,2,1,0:T(8,128)S(1)} %get-tuple-element.89, f32[1,32,8,512]{3,2,1,0:T(8,128)S(1)} %get-tuple-element.90, f32[1,32,8,512]{3,2,1,0:T(8,128)S(1)} %get-tuple-element.91, f32[1,32,8,512]{3,2,1,0:T(8,128)S(1)} %get-tuple-element.92, ...), kind=kLoop, calls=%fused_computation.33 | loop fusion | flops 13074432 | bytes 26779648 | tf_op jit(solution)/shard_map/transpose(jvp())/add_any | solution.py:122
  74.6 0.4 collective-permute-start.5
  75.2 1.8 %collective-permute-start.4 = (bf16[1,32,3,512]{3,2,1,0:T(4,128)(2,1)S(1)}, bf16[1,32,3,512]{3,2,1,0:T(4,128)(2,1)S(1)}, u32[]{:S(2)}, u32[]{:S(2)}) collective-permute-start(bf16[1,32,3,512]{3,2,1,0:T(4,128)(2,1)S(1)} %fusion.96), channel_id=1, source_target_pairs={{0,4},{4,8},{8,12},{12,16},{16,20},{20,24},{24,28},{28,32},{32,36}... | collective-permute-start | bytes 294920 | tf_op jit(solution)/shard_map/ppermute | solution.py:20
  77.0 15.7 %collective-permute-done.7 = bf16[1088,512]{1,0:T(8,128)(2,1)S(1)} collective-permute-done((bf16[1088,512]{1,0:T(8,128)(2,1)S(1)}, bf16[1088,512]{1,0:T(8,128)(2,1)S(1)}, u32[]{:S(2)}, u32[]{:S(2)}) %collective-permute-start.7) | collective-permute-done | bytes 1114144 | tf_op jit(solution)/shard_map/ppermute | solution.py:31
  93.2 1.0 collective-permute-start.8
  94.2 1.1 collective-permute-start.10
  95.3 1.4 collective-permute-start.9
  96.7 1.4 fusion.9
  98.1 6.2 %collective-permute-done.8 = bf16[272,512]{1,0:T(8,128)(2,1)S(1)} collective-permute-done((bf16[272,512]{1,0:T(8,128)(2,1)S(1)}, bf16[272,512]{1,0:T(8,128)(2,1)S(1)}, u32[]{:S(2)}, u32[]{:S(2)}) %collective-permute-start.8) | collective-permute-done | bytes 278560 | tf_op jit(solution)/shard_map/ppermute | solution.py:85
  104.3 4.5 %collective-permute-done.10 = bf16[272,512]{1,0:T(8,128)(2,1)S(1)} collective-permute-done((bf16[272,512]{1,0:T(8,128)(2,1)S(1)}, bf16[272,512]{1,0:T(8,128)(2,1)S(1)}, u32[]{:S(2)}, u32[]{:S(2)}) %collective-permute-start.10) | collective-permute-done | bytes 278560 | tf_op jit(solution)/shard_map/ppermute | solution.py:85
  109.0 3.4 %collective-permute-start.11 = (bf16[68,512]{1,0:T(8,128)(2,1)S(1)}, bf16[68,512]{1,0:T(8,128)(2,1)S(1)}, u32[]{:S(2)}, u32[]{:S(2)}) collective-permute-start(bf16[68,512]{1,0:T(8,128)(2,1)S(1)} %get-tuple-element.84), channel_id=1, source_target_pairs={{0,32},{4,36},{8,40},{12,44},{16,48},{20,52},{24,56},{28,60},{32,0... | collective-permute-start | bytes 208904 | tf_op jit(solution)/shard_map/ppermute | solution.py:85
  112.4 7.8 %collective-permute-start.13 = (bf16[68,512]{1,0:T(8,128)(2,1)S(1)}, bf16[68,512]{1,0:T(8,128)(2,1)S(1)}, u32[]{:S(2)}, u32[]{:S(2)}) collective-permute-start(bf16[68,512]{1,0:T(8,128)(2,1)S(1)} %get-tuple-element.85), channel_id=1, source_target_pairs={{0,48},{4,52},{8,56},{12,60},{16,32},{20,36},{24,40},{28,44},{32,1... | collective-permute-start | bytes 208904 | tf_op jit(solution)/shard_map/ppermute | solution.py:85
  120.3 5.0 %collective-permute-done.13 = bf16[68,512]{1,0:T(8,128)(2,1)S(1)} collective-permute-done((bf16[68,512]{1,0:T(8,128)(2,1)S(1)}, bf16[68,512]{1,0:T(8,128)(2,1)S(1)}, u32[]{:S(2)}, u32[]{:S(2)}) %collective-permute-start.13) | collective-permute-done | bytes 69664 | tf_op jit(solution)/shard_map/ppermute | solution.py:85
  125.4 3.2 %collective-permute-start.16 = (bf16[68,512]{1,0:T(8,128)(2,1)S(1)}, bf16[68,512]{1,0:T(8,128)(2,1)S(1)}, u32[]{:S(2)}, u32[]{:S(2)}) collective-permute-start(bf16[68,512]{1,0:T(8,128)(2,1)S(1)} %add_convert_fusion.1), channel_id=1, source_target_pairs={{0,192},{4,196},{8,200},{12,204},{16,208},{20,212},{24,216},{28,22... | collective-permute-start | bytes 208904 | tf_op jit(solution)/shard_map/ppermute | solution.py:85
  128.6 3.3 %collective-permute-start.15 = (bf16[68,512]{1,0:T(8,128)(2,1)S(1)}, bf16[68,512]{1,0:T(8,128)(2,1)S(1)}, u32[]{:S(2)}, u32[]{:S(2)}) collective-permute-start(bf16[68,512]{1,0:T(8,128)(2,1)S(1)} %add_convert_fusion.1), channel_id=1, source_target_pairs={{0,64},{4,68},{8,72},{12,76},{16,80},{20,84},{24,88},{28,92},{32,9... | collective-permute-start | bytes 208904 | tf_op jit(solution)/shard_map/ppermute | solution.py:85
  131.9 2.7 %collective-permute-start.14 = (bf16[68,512]{1,0:T(8,128)(2,1)S(1)}, bf16[68,512]{1,0:T(8,128)(2,1)S(1)}, u32[]{:S(2)}, u32[]{:S(2)}) collective-permute-start(bf16[68,512]{1,0:T(8,128)(2,1)S(1)} %add_convert_fusion.1), channel_id=1, source_target_pairs={{0,128},{4,132},{8,136},{12,140},{16,144},{20,148},{24,152},{28,15... | collective-permute-start | bytes 208904 | tf_op jit(solution)/shard_map/ppermute | solution.py:85
  134.8 4.4 %collective-permute-done.16 = bf16[68,512]{1,0:T(8,128)(2,1)S(1)} collective-permute-done((bf16[68,512]{1,0:T(8,128)(2,1)S(1)}, bf16[68,512]{1,0:T(8,128)(2,1)S(1)}, u32[]{:S(2)}, u32[]{:S(2)}) %collective-permute-start.16) | collective-permute-done | bytes 69664 | tf_op jit(solution)/shard_map/ppermute | solution.py:85
  139.3 1.1 collective-permute-start.18
  140.5 2.3 %collective-permute-start.17 = (bf16[68,512]{1,0:T(8,128)(2,1)S(1)}, bf16[68,512]{1,0:T(8,128)(2,1)S(1)}, u32[]{:S(2)}, u32[]{:S(2)}) collective-permute-start(bf16[68,512]{1,0:T(8,128)(2,1)S(1)} %fusion.113), channel_id=1, source_target_pairs={{0,32},{4,36},{8,40},{12,44},{16,48},{20,52},{24,56},{28,60},{32,0... | collective-permute-start | bytes 208904 | tf_op jit(solution)/shard_map/ppermute | solution.py:85
  143.0 0.7 dynamic_update_slice.24
  143.7 3.7 %collective-permute-done.17 = bf16[68,512]{1,0:T(8,128)(2,1)S(1)} collective-permute-done((bf16[68,512]{1,0:T(8,128)(2,1)S(1)}, bf16[68,512]{1,0:T(8,128)(2,1)S(1)}, u32[]{:S(2)}, u32[]{:S(2)}) %collective-permute-start.17) | collective-permute-done | bytes 69664 | tf_op jit(solution)/shard_map/ppermute | solution.py:85
  147.4 0.4 dynamic_update_slice.25
  147.8 0.7 dynamic_update_slice.26
  148.5 0.7 dynamic_update_slice.27
  149.2 0.8 collective-permute-start.20
  150.4 2.0 %collective-permute-start.21 = (bf16[272,512]{1,0:T(8,128)(2,1)S(1)}, bf16[272,512]{1,0:T(8,128)(2,1)S(1)}, u32[]{:S(2)}, u32[]{:S(2)}) collective-permute-start(bf16[272,512]{1,0:T(8,128)(2,1)S(1)} %dynamic_update_slice.27), channel_id=1, source_target_pairs={{0,4},{4,0},{8,12},{12,8},{16,20},{20,16},{24,28},{28,24},{32,36},... | collective-permute-start | bytes 835592 | tf_op jit(solution)/shard_map/ppermute | solution.py:85
  152.4 0.9 pad_maximum_fusion.10
  153.3 1.4 collective-permute-start.22
  154.9 5.5 %collective-permute-done.20 = bf16[272,512]{1,0:T(8,128)(2,1)S(1)} collective-permute-done((bf16[272,512]{1,0:T(8,128)(2,1)S(1)}, bf16[272,512]{1,0:T(8,128)(2,1)S(1)}, u32[]{:S(2)}, u32[]{:S(2)}) %collective-permute-start.20) | collective-permute-done | bytes 278560 | tf_op jit(solution)/shard_map/ppermute | solution.py:85
  160.4 1.7 %collective-permute-done.21 = bf16[272,512]{1,0:T(8,128)(2,1)S(1)} collective-permute-done((bf16[272,512]{1,0:T(8,128)(2,1)S(1)}, bf16[272,512]{1,0:T(8,128)(2,1)S(1)}, u32[]{:S(2)}, u32[]{:S(2)}) %collective-permute-start.21) | collective-permute-done | bytes 278560 | tf_op jit(solution)/shard_map/ppermute | solution.py:85
  162.1 1.7 %collective-permute-done.22 = bf16[272,512]{1,0:T(8,128)(2,1)S(1)} collective-permute-done((bf16[272,512]{1,0:T(8,128)(2,1)S(1)}, bf16[272,512]{1,0:T(8,128)(2,1)S(1)}, u32[]{:S(2)}, u32[]{:S(2)}) %collective-permute-start.22) | collective-permute-done | bytes 278560 | tf_op jit(solution)/shard_map/ppermute | solution.py:85
  163.8 0.6 slice.896
  164.4 0.7 slice.895
  165.1 1.6 fusion.121
  (94 shorter events, 7.2 us)
Async XLA Ops:
  0.6 12.9 %copy-start.2 = (bf16[1,32,8,512]{3,2,1,0:T(8,128)(2,1)S(1)}, bf16[1,32,8,512]{3,2,1,0:T(8,128)(2,1)}, u32[]{:S(2)}) copy-start(bf16[1,32,8,512]{3,2,1,0:T(8,128)(2,1)} %param.7) | copy-start | bytes 786436
  0.6 9.3 %copy-start.8 = (f32[49,512]{1,0:T(8,128)S(1)}, f32[49,512]{1,0:T(8,128)}, u32[]{:S(2)}) copy-start(f32[49,512]{1,0:T(8,128)} %param.9) | copy-start | bytes 301060
  0.7 9.4 %copy-start.10 = (s32[1,2]{1,0:T(1,128)S(1)}, s32[1,2]{1,0:T(1,128)}, u32[]{:S(2)}) copy-start(s32[1,2]{1,0:T(1,128)} %param.8) | copy-start | bytes 28
  1.8 11.4 %collective-permute-start.1 = (bf16[1,32,3,512]{3,2,1,0:T(4,128)(2,1)S(1)}, bf16[1,32,3,512]{3,2,1,0:T(4,128)(2,1)S(1)}, u32[]{:S(2)}, u32[]{:S(2)}) collective-permute-start(bf16[1,32,3,512]{3,2,1,0:T(4,128)(2,1)S(1)} %get-tuple-element.136), channel_id=1, source_target_pairs={{0,4},{4,8},{8,12},{12,16},{16,20},{20,24},{24,28},{28,32},{32,36}... | collective-permute-start | bytes 294920 | tf_op jit(solution)/shard_map/ppermute | solution.py:20
  3.4 9.9 %collective-permute-start.2 = (bf16[1,32,3,512]{3,2,1,0:T(4,128)(2,1)S(1)}, bf16[1,32,3,512]{3,2,1,0:T(4,128)(2,1)S(1)}, u32[]{:S(2)}, u32[]{:S(2)}) collective-permute-start(bf16[1,32,3,512]{3,2,1,0:T(4,128)(2,1)S(1)} %get-tuple-element.137), channel_id=1, source_target_pairs={{4,0},{8,4},{12,8},{16,12},{20,16},{24,20},{28,24},{32,28},{36,32}... | collective-permute-start | bytes 294920 | tf_op jit(solution)/shard_map/ppermute | solution.py:22
  8.3 24.7 %collective-permute-start = (bf16[2,512,512]{2,1,0:T(8,128)(2,1)}, bf16[2,512,512]{2,1,0:T(8,128)(2,1)}, u32[]{:S(2)}, u32[]{:S(2)}) collective-permute-start(bf16[2,512,512]{2,1,0:T(8,128)(2,1)} %pad_maximum_fusion.4), channel_id=1, source_target_pairs={{0,2},{1,3},{2,0},{3,1},{4,6},{5,7},{6,4},{7,5},{8,10},{9,11},{10,... | collective-permute-start | bytes 3145736 | tf_op jit(solution)/shard_map/ppermute | solution.py:31
  13.8 4.9 %copy-start.9 = (f32[512]{0:T(512)S(1)}, f32[512]{0:T(512)}, u32[]{:S(2)}) copy-start(f32[512]{0:T(512)} %param.10) | copy-start | bytes 6148
  13.8 19.2 %copy-start.5 = (bf16[512,512]{1,0:T(8,128)(2,1)S(1)}, bf16[512,512]{1,0:T(8,128)(2,1)}, u32[]{:S(2)}) copy-start(bf16[512,512]{1,0:T(8,128)(2,1)} %param.12) | copy-start | bytes 1572868
  36.0 4.5 %collective-permute-start.3 = (bf16[2,2,512,512]{3,2,1,0:T(8,128)(2,1)}, bf16[2,2,512,512]{3,2,1,0:T(8,128)(2,1)}, u32[]{:S(2)}, u32[]{:S(2)}) collective-permute-start(bf16[2,2,512,512]{3,2,1,0:T(8,128)(2,1)} %pad_maximum_fusion.2), channel_id=1, source_target_pairs={{0,1},{1,0},{2,3},{3,2},{4,5},{5,4},{6,7},{7,6},{8,9},{9,8},{10,11... | collective-permute-start | bytes 6291464 | tf_op jit(solution)/shard_map/ppermute | solution.py:31
  43.6 1.4 copy-start.3
  43.8 1.2 copy-start.1
  44.5 9.0 %copy-start.6 = (bf16[256,2048]{1,0:T(8,128)(2,1)}, bf16[256,2048]{1,0:T(8,128)(2,1)S(1)}, u32[]{:S(2)}) copy-start(bf16[256,2048]{1,0:T(8,128)(2,1)S(1)} %get-tuple-element.189) | copy-start | bytes 3145732
  55.7 2.8 %copy-start = (bf16[2,2,1088,512]{3,2,1,0:T(8,128)(2,1)}, bf16[2,2,1088,512]{3,2,1,0:T(8,128)(2,1)S(1)}, u32[]{:S(2)}) copy-start(bf16[2,2,1088,512]{3,2,1,0:T(8,128)(2,1)S(1)} %pad_maximum_fusion) | copy-start | bytes 13369348
  58.5 4.9 %collective-permute-start.6 = (bf16[2176,512]{1,0:T(8,128)(2,1)}, bf16[2176,512]{1,0:T(8,128)(2,1)}, u32[]{:S(2)}, u32[]{:S(2)}) collective-permute-start(bf16[2176,512]{1,0:T(8,128)(2,1)} %constant_dynamic-slice_fusion), channel_id=1, source_target_pairs={{0,1},{1,0},{2,3},{3,2},{4,5},{5,4},{6,7},{7,6},{8,9},{9,8},{10,11... | collective-permute-start | bytes 6684680 | tf_op jit(solution)/shard_map/ppermute | solution.py:31
  60.8 2.6 %slice-start = ((s8[4456448]{0:T(1024)(128)(4,1)}), s8[4194304]{0:T(1024)(128)(4,1)S(1)}, s32[]{:S(2)}) async-start(s8[4456448]{0:T(1024)(128)(4,1)} %bitcast.305), calls=%async_computation | async-start | bytes 8388608
  62.1 1.3 slice-start.1
  65.8 26.9 %collective-permute-start.7 = (bf16[1088,512]{1,0:T(8,128)(2,1)S(1)}, bf16[1088,512]{1,0:T(8,128)(2,1)S(1)}, u32[]{:S(2)}, u32[]{:S(2)}) collective-permute-start(bf16[1088,512]{1,0:T(8,128)(2,1)S(1)} %dynamic-slice_convert_fusion), channel_id=1, source_target_pairs={{0,2},{1,3},{2,0},{3,1},{4,6},{5,7},{6,4},{7,5},{8,10},{9,11},{10,... | collective-permute-start | bytes 3342344 | tf_op jit(solution)/shard_map/ppermute | solution.py:31
  74.6 75.4 %collective-permute-start.5 = (bf16[1,32,3,512]{3,2,1,0:T(4,128)(2,1)S(1)}, bf16[1,32,3,512]{3,2,1,0:T(4,128)(2,1)S(1)}, u32[]{:S(2)}, u32[]{:S(2)}) collective-permute-start(bf16[1,32,3,512]{3,2,1,0:T(4,128)(2,1)S(1)} %fusion.97), channel_id=1, source_target_pairs={{4,0},{8,4},{12,8},{16,12},{20,16},{24,20},{28,24},{32,28},{36,32}... | collective-permute-start | bytes 294920 | tf_op jit(solution)/shard_map/ppermute | solution.py:22
  75.1 21.6 %copy-start.4 = (bf16[4,1,512,512]{3,2,1,0:T(8,128)(2,1)S(1)}, bf16[4,1,512,512]{3,2,1,0:T(8,128)(2,1)}, u32[]{:S(2)}) copy-start(bf16[4,1,512,512]{3,2,1,0:T(8,128)(2,1)} %copy-done.3) | copy-start | bytes 6291460
  75.1 21.6 %copy-start.7 = (bf16[256,2048]{1,0:T(8,128)(2,1)S(1)}, bf16[256,2048]{1,0:T(8,128)(2,1)}, u32[]{:S(2)}) copy-start(bf16[256,2048]{1,0:T(8,128)(2,1)} %copy-done.6) | copy-start | bytes 3145732
  75.2 74.9 %collective-permute-start.4 = (bf16[1,32,3,512]{3,2,1,0:T(4,128)(2,1)S(1)}, bf16[1,32,3,512]{3,2,1,0:T(4,128)(2,1)S(1)}, u32[]{:S(2)}, u32[]{:S(2)}) collective-permute-start(bf16[1,32,3,512]{3,2,1,0:T(4,128)(2,1)S(1)} %fusion.96), channel_id=1, source_target_pairs={{0,4},{4,8},{8,12},{12,16},{16,20},{20,24},{24,28},{28,32},{32,36}... | collective-permute-start | bytes 294920 | tf_op jit(solution)/shard_map/ppermute | solution.py:20
  93.2 11.2 %collective-permute-start.8 = (bf16[272,512]{1,0:T(8,128)(2,1)S(1)}, bf16[272,512]{1,0:T(8,128)(2,1)S(1)}, u32[]{:S(2)}, u32[]{:S(2)}) collective-permute-start(bf16[272,512]{1,0:T(8,128)(2,1)S(1)} %get-tuple-element.73), channel_id=1, source_target_pairs={{0,8},{4,12},{8,0},{12,4},{16,24},{20,28},{24,16},{28,20},{32,40},... | collective-permute-start | bytes 835592 | tf_op jit(solution)/shard_map/ppermute | solution.py:85
  94.2 14.6 %collective-permute-start.10 = (bf16[272,512]{1,0:T(8,128)(2,1)S(1)}, bf16[272,512]{1,0:T(8,128)(2,1)S(1)}, u32[]{:S(2)}, u32[]{:S(2)}) collective-permute-start(bf16[272,512]{1,0:T(8,128)(2,1)S(1)} %get-tuple-element.74), channel_id=1, source_target_pairs={{0,12},{4,8},{8,4},{12,0},{16,28},{20,24},{24,20},{28,16},{32,44},... | collective-permute-start | bytes 835592 | tf_op jit(solution)/shard_map/ppermute | solution.py:85
  95.3 13.5 %collective-permute-start.9 = (bf16[272,512]{1,0:T(8,128)(2,1)S(1)}, bf16[272,512]{1,0:T(8,128)(2,1)S(1)}, u32[]{:S(2)}, u32[]{:S(2)}) collective-permute-start(bf16[272,512]{1,0:T(8,128)(2,1)S(1)} %get-tuple-element.75), channel_id=1, source_target_pairs={{0,4},{4,0},{8,12},{12,8},{16,20},{20,16},{24,28},{28,24},{32,36},... | collective-permute-start | bytes 835592 | tf_op jit(solution)/shard_map/ppermute | solution.py:85
  109.0 11.3 %collective-permute-start.11 = (bf16[68,512]{1,0:T(8,128)(2,1)S(1)}, bf16[68,512]{1,0:T(8,128)(2,1)S(1)}, u32[]{:S(2)}, u32[]{:S(2)}) collective-permute-start(bf16[68,512]{1,0:T(8,128)(2,1)S(1)} %get-tuple-element.84), channel_id=1, source_target_pairs={{0,32},{4,36},{8,40},{12,44},{16,48},{20,52},{24,56},{28,60},{32,0... | collective-permute-start | bytes 208904 | tf_op jit(solution)/shard_map/ppermute | solution.py:85
  112.4 13.0 %collective-permute-start.13 = (bf16[68,512]{1,0:T(8,128)(2,1)S(1)}, bf16[68,512]{1,0:T(8,128)(2,1)S(1)}, u32[]{:S(2)}, u32[]{:S(2)}) collective-permute-start(bf16[68,512]{1,0:T(8,128)(2,1)S(1)} %get-tuple-element.85), channel_id=1, source_target_pairs={{0,48},{4,52},{8,56},{12,60},{16,32},{20,36},{24,40},{28,44},{32,1... | collective-permute-start | bytes 208904 | tf_op jit(solution)/shard_map/ppermute | solution.py:85
  120.2 5.1 %collective-permute-start.12 = (bf16[68,512]{1,0:T(8,128)(2,1)S(1)}, bf16[68,512]{1,0:T(8,128)(2,1)S(1)}, u32[]{:S(2)}, u32[]{:S(2)}) collective-permute-start(bf16[68,512]{1,0:T(8,128)(2,1)S(1)} %get-tuple-element.86), channel_id=1, source_target_pairs={{0,16},{4,20},{8,24},{12,28},{16,0},{20,4},{24,8},{28,12},{32,48},... | collective-permute-start | bytes 208904 | tf_op jit(solution)/shard_map/ppermute | solution.py:85
  125.4 13.7 %collective-permute-start.16 = (bf16[68,512]{1,0:T(8,128)(2,1)S(1)}, bf16[68,512]{1,0:T(8,128)(2,1)S(1)}, u32[]{:S(2)}, u32[]{:S(2)}) collective-permute-start(bf16[68,512]{1,0:T(8,128)(2,1)S(1)} %add_convert_fusion.1), channel_id=1, source_target_pairs={{0,192},{4,196},{8,200},{12,204},{16,208},{20,212},{24,216},{28,22... | collective-permute-start | bytes 208904 | tf_op jit(solution)/shard_map/ppermute | solution.py:85
  128.6 10.5 %collective-permute-start.15 = (bf16[68,512]{1,0:T(8,128)(2,1)S(1)}, bf16[68,512]{1,0:T(8,128)(2,1)S(1)}, u32[]{:S(2)}, u32[]{:S(2)}) collective-permute-start(bf16[68,512]{1,0:T(8,128)(2,1)S(1)} %add_convert_fusion.1), channel_id=1, source_target_pairs={{0,64},{4,68},{8,72},{12,76},{16,80},{20,84},{24,88},{28,92},{32,9... | collective-permute-start | bytes 208904 | tf_op jit(solution)/shard_map/ppermute | solution.py:85
  131.9 7.3 %collective-permute-start.14 = (bf16[68,512]{1,0:T(8,128)(2,1)S(1)}, bf16[68,512]{1,0:T(8,128)(2,1)S(1)}, u32[]{:S(2)}, u32[]{:S(2)}) collective-permute-start(bf16[68,512]{1,0:T(8,128)(2,1)S(1)} %add_convert_fusion.1), channel_id=1, source_target_pairs={{0,128},{4,132},{8,136},{12,140},{16,144},{20,148},{24,152},{28,15... | collective-permute-start | bytes 208904 | tf_op jit(solution)/shard_map/ppermute | solution.py:85
  139.2 9.3 %collective-permute-start.19 = (bf16[68,512]{1,0:T(8,128)(2,1)S(1)}, bf16[68,512]{1,0:T(8,128)(2,1)S(1)}, u32[]{:S(2)}, u32[]{:S(2)}) collective-permute-start(bf16[68,512]{1,0:T(8,128)(2,1)S(1)} %fusion.113), channel_id=1, source_target_pairs={{0,48},{4,52},{8,56},{12,60},{16,32},{20,36},{24,40},{28,44},{32,1... | collective-permute-start | bytes 208904 | tf_op jit(solution)/shard_map/ppermute | solution.py:85
  139.3 8.5 %collective-permute-start.18 = (bf16[68,512]{1,0:T(8,128)(2,1)S(1)}, bf16[68,512]{1,0:T(8,128)(2,1)S(1)}, u32[]{:S(2)}, u32[]{:S(2)}) collective-permute-start(bf16[68,512]{1,0:T(8,128)(2,1)S(1)} %fusion.113), channel_id=1, source_target_pairs={{0,16},{4,20},{8,24},{12,28},{16,0},{20,4},{24,8},{28,12},{32,48},... | collective-permute-start | bytes 208904 | tf_op jit(solution)/shard_map/ppermute | solution.py:85
  140.5 6.9 %collective-permute-start.17 = (bf16[68,512]{1,0:T(8,128)(2,1)S(1)}, bf16[68,512]{1,0:T(8,128)(2,1)S(1)}, u32[]{:S(2)}, u32[]{:S(2)}) collective-permute-start(bf16[68,512]{1,0:T(8,128)(2,1)S(1)} %fusion.113), channel_id=1, source_target_pairs={{0,32},{4,36},{8,40},{12,44},{16,48},{20,52},{24,56},{28,60},{32,0... | collective-permute-start | bytes 208904 | tf_op jit(solution)/shard_map/ppermute | solution.py:85
  149.2 11.1 %collective-permute-start.20 = (bf16[272,512]{1,0:T(8,128)(2,1)S(1)}, bf16[272,512]{1,0:T(8,128)(2,1)S(1)}, u32[]{:S(2)}, u32[]{:S(2)}) collective-permute-start(bf16[272,512]{1,0:T(8,128)(2,1)S(1)} %dynamic_update_slice.27), channel_id=1, source_target_pairs={{0,8},{4,12},{8,0},{12,4},{16,24},{20,28},{24,16},{28,20},{32,40},... | collective-permute-start | bytes 835592 | tf_op jit(solution)/shard_map/ppermute | solution.py:85
  150.4 11.7 %collective-permute-start.21 = (bf16[272,512]{1,0:T(8,128)(2,1)S(1)}, bf16[272,512]{1,0:T(8,128)(2,1)S(1)}, u32[]{:S(2)}, u32[]{:S(2)}) collective-permute-start(bf16[272,512]{1,0:T(8,128)(2,1)S(1)} %dynamic_update_slice.27), channel_id=1, source_target_pairs={{0,4},{4,0},{8,12},{12,8},{16,20},{20,16},{24,28},{28,24},{32,36},... | collective-permute-start | bytes 835592 | tf_op jit(solution)/shard_map/ppermute | solution.py:85
  153.3 10.5 %collective-permute-start.22 = (bf16[272,512]{1,0:T(8,128)(2,1)S(1)}, bf16[272,512]{1,0:T(8,128)(2,1)S(1)}, u32[]{:S(2)}, u32[]{:S(2)}) collective-permute-start(bf16[272,512]{1,0:T(8,128)(2,1)S(1)} %dynamic_update_slice.27), channel_id=1, source_target_pairs={{0,12},{4,8},{8,4},{12,0},{16,28},{20,24},{24,20},{28,16},{32,44},... | collective-permute-start | bytes 835592 | tf_op jit(solution)/shard_map/ppermute | solution.py:85
where the time goes:
time: 169 us; the launch traced here: 167 us
  waiting for transfers between devices  66.9 us (40%)
  starting transfers between devices  41.6 us (25%)
  other arithmetic  33.6 us (20%)
  local copies, waits for them, and re-layouts  12.4 us (7%)
  matrix products  6.92 us (4%)
  between operations  5.21 us (3%)
    ppermute x4, waiting for transfers between devices, exchange(): return lax.ppermute(value, axis, [(i, i ^ 1 << bit) for i in range(count)])  34.3 us
    ppermute x15, waiting for transfers between devices, swapped(): return lax.ppermute(value, axis, [(i, i ^ mask) for i in range(count)])  32.6 us
    ppermute x15, starting transfers between devices, swapped(): return lax.ppermute(value, axis, [(i, i ^ mask) for i in range(count)])  31.8 us
    add_any x1, other arithmetic, depthwise(): padded[:, row:row + height, col:col + width, :] * kernel[7 * row + col]  6.73 us
    reduce_sum x1, other arithmetic, body(): mean = jnp.mean(rows, axis=-1, keepdims=True)  4.43 us
    reduce_sum x3, other arithmetic, depthwise(): padded[:, row:row + height, col:col + width, :] * kernel[7 * row + col]  4.1 us
    ppermute x2, starting transfers between devices, extended(): lax.ppermute(tail, axis, [(i, (i + 1) % count) for i in range(count)])  3.39 us
    ppermute x4, starting transfers between devices, exchange(): return lax.ppermute(value, axis, [(i, i ^ 1 << bit) for i in range(count)])  3.38 us
  transfers between devices with their start and end apart: 23, of which 11 were waited for; matrix products, arithmetic and copies ran while one was open for 15% of the time, Pallas kernels for 0%

commit v1 on v0

--- a/solution.py
+++ b/solution.py
@@ -85,9 +85,11 @@
     return lax.ppermute(value, axis, [(i, i ^ mask) for i in range(count)])
 
 
-def gathered(shard, anchor):
+def gathered(shard, anchor, after=None):
     me = lax.axis_index("fsdp")
     high, low = (me >> 1) & 1, me & 1
+    if after is not None:
+        shard, after = lax.optimization_barrier((shard, after))
     got = exchange(shard, "fsdp", 1)
     pair = jnp.stack([jnp.where(high == 0, shard, got), jnp.where(high == 0, got, shard)])
     pair, anchor = lax.optimization_barrier((pair, anchor))
@@ -147,9 +149,10 @@
     scaled = (normed * gain).astype(jnp.bfloat16)
     back = cotangent.reshape(count, channels)
     contract_last = (((1,), (1,)), ((), ()))
-    both, scaled = gathered(jnp.stack([w_in, w_out]), scaled)
-    full_in = jnp.concatenate([both[f, 0] for f in range(both.shape[0])], axis=1)
-    full_out = both[:, 1].reshape(-1, w_out.shape[1])
+    in4, scaled = gathered(w_in, scaled)
+    out4, _ = gathered(w_out, back, after=in4)
+    full_in = jnp.concatenate([in4[f] for f in range(in4.shape[0])], axis=1)
+    full_out = out4.reshape(-1, w_out.shape[1])
     pre = jnp.dot(scaled, full_in, preferred_element_type=jnp.float32)
     hidden = gelu(pre).astype(jnp.bfloat16)
     branch = jnp.dot(hidden, full_out, preferred_element_type=jnp.float32)

time: 169 us -> 171 us (1.012)
  local copies, waits for them, and re-layouts: 12.4 us -> 17.6 us
  waiting for transfers between devices: 66.9 us -> 64.1 us
    ppermute x4 -> x6, waiting for transfers between devices: 34.3 us -> 30.9 us  [exchange(): return lax.ppermute(value, axis, [(i, i ^ 1 << bit) for i in range(count)])]
    slice x3, local copies, waits for them, and re-layouts: 0.08 us -> 3.19 us  [depthwise(): kernel[7 * row + col]]
    another operation x4 -> x3, other arithmetic: 2.8 us -> 0.54 us  [the longest x1 2.27 us: body(): both, scaled = gathered(jnp.stack([w_in, w_out]), scaled)]
    another operation x2 -> x4, other arithmetic: 2.88 us -> 3.55 us  [gathered(): jnp.stack([first, second], axis=1).reshape((4,) + shard.shape)]
    another operation x2 -> x4, other arithmetic: 3.03 us -> 3.55 us  [gathered(): jnp.stack([jnp.where(high == 0, shard, got), jnp.where(high == 0, got, sh...]
    ppermute x4 -> x6, starting transfers between devices: 3.38 us -> 3.79 us  [exchange(): return lax.ppermute(value, axis, [(i, i ^ 1 << bit) for i in range(count)])]
  transfers between devices with their start and end apart: 23 -> 25, of which waited for: 11 -> 12; matrix products, arithmetic and copies ran while one was open for 15% -> 19% of each run, Pallas kernels for 0% -> 0%
where the time goes in v1:
time: 171 us; the launch traced here: 169 us
  waiting for transfers between devices  64.1 us (37%)
  starting transfers between devices  42.1 us (25%)
  other arithmetic  32.8 us (19%)
  local copies, waits for them, and re-layouts  17.6 us (10%)
  matrix products  6.98 us (4%)
  between operations  5.22 us (3%)
    ppermute x15, waiting for transfers between devices, swapped(): return lax.ppermute(value, axis, [(i, i ^ mask) for i in range(count)])  33.3 us
    ppermute x15, starting transfers between devices, swapped(): return lax.ppermute(value, axis, [(i, i ^ mask) for i in range(count)])  31.9 us
    ppermute x6, waiting for transfers between devices, exchange(): return lax.ppermute(value, axis, [(i, i ^ 1 << bit) for i in range(count)])  30.9 us
    add_any x1, other arithmetic, depthwise(): padded[:, row:row + height, col:col + width, :] * kernel[7 * row + col]  6.75 us
    reduce_sum x1, other arithmetic, body(): mean = jnp.mean(rows, axis=-1, keepdims=True)  4.42 us
    reduce_sum x3, other arithmetic, depthwise(): padded[:, row:row + height, col:col + width, :] * kernel[7 * row + col]  4.1 us
    ppermute x6, starting transfers between devices, exchange(): return lax.ppermute(value, axis, [(i, i ^ 1 << bit) for i in range(count)])  3.79 us
    another operation x4, other arithmetic, gathered(): jnp.stack([jnp.where(high == 0, shard, got), jnp.where(high == 0, got, sh...  3.55 us
  transfers between devices with their start and end apart: 25, of which 12 were waited for; matrix products, arithmetic and copies ran while one was open for 19% of the time, Pallas kernels for 0%

profile of v1, /device:TPU:32, one launch (start us, length us, event | category | flops | bytes accessed | tf_op | source)
XLA Modules:
  0.0 168.8 jit_solution(10242511173663023998)
XLA Ops:
  0.6 1.2 fusion.122
  1.8 1.6 collective-permute-start.1
  3.4 2.6 %collective-permute-start.2 = (bf16[1,32,3,512]{3,2,1,0:T(4,128)(2,1)S(1)}, bf16[1,32,3,512]{3,2,1,0:T(4,128)(2,1)S(1)}, u32[]{:S(2)}, u32[]{:S(2)}) collective-permute-start(bf16[1,32,3,512]{3,2,1,0:T(4,128)(2,1)S(1)} %get-tuple-element.145), channel_id=1, source_target_pairs={{4,0},{8,4},{12,8},{16,12},{20,16},{24,20},{28,24},{32,28},{36,32}... | collective-permute-start | bytes 294920 | tf_op jit(solution)/shard_map/ppermute | solution.py:22
  6.1 1.6 collective-permute-start
  7.6 1.0 fusion.125
  8.6 1.1 fusion.123
  9.7 1.1 fusion.124
  10.8 1.3 fusion.126
  15.4 4.4 %fusion.118 = (f32[32,8]{1,0:T(8,128)S(1)}, f32[1,32,8,512]{3,2,1,0:T(8,128)S(1)}) fusion(f32[512]{0:T(512)S(1)} %bitcast.341, bf16[1,38,14,512]{3,2,1,0:T(8,128)(2,1)S(1)} %get-tuple-element.68, f32[512]{0:T(512)S(1)} %bitcast.359, f32[512]{0:T(512)S(1)} %bitcast.395, f32[512]{0:T(512)S(1)} %bitcast.397, f32[512]{0:T(512)S(1)} %bitcast.399, ...), kind=kLoop, calls=%fused_computation.308 | loop fusion | flops 21626624 | bytes 12094464 | tf_op jit(solution)/shard_map/reduce_sum | solution.py:145
  20.4 1.3 select_bitcast_fusion.7
  21.6 1.1 pad_maximum_fusion.4
  22.7 3.0 %collective-permute-done.3 = bf16[2,512,512]{2,1,0:T(8,128)(2,1)} collective-permute-done((bf16[2,512,512]{2,1,0:T(8,128)(2,1)}, bf16[2,512,512]{2,1,0:T(8,128)(2,1)}, u32[]{:S(2)}, u32[]{:S(2)}) %collective-permute-start.3) | collective-permute-done | bytes 1048608 | tf_op jit(solution)/shard_map/ppermute | solution.py:31
  25.7 1.7 select_bitcast_fusion.3
  27.4 1.5 pad_maximum_fusion.1
  28.9 0.7 collective-permute-start.4
  29.7 1.7 %slice_bitcast_fusion.3 = (bf16[512,512]{1,0:T(8,128)(2,1)S(1)}, bf16[512,512]{1,0:T(8,128)(2,1)S(1)}, bf16[512,512]{1,0:T(8,128)(2,1)S(1)}, bf16[512,512]{1,0:T(8,128)(2,1)S(1)}) fusion(bf16[4,512,512]{2,1,0:T(8,128)(2,1)} %bitcast.316), kind=kLoop, calls=%fused_computation.190 | loop fusion | bytes 4194304 | tf_op jit(solution)/shard_map/squeeze | solution.py:154
  31.4 11.6 %collective-permute-done.4 = bf16[512,512]{1,0:T(8,128)(2,1)} collective-permute-done((bf16[512,512]{1,0:T(8,128)(2,1)S(1)}, bf16[512,512]{1,0:T(8,128)(2,1)}, u32[]{:S(2)}, u32[]{:S(2)}) %collective-permute-start.4) | collective-permute-done | bytes 524320 | tf_op jit(solution)/shard_map/ppermute | solution.py:31
  43.0 1.1 select_bitcast_fusion.5
  44.5 0.8 multiply_convert_fusion
  46.8 0.6 fusion.1
  47.9 1.3 fusion.3
  49.3 0.9 multiply_reduce_fusion
  50.2 2.1 %fusion.86 = (f32[512]{0:T(512)S(1)}, f32[512]{0:T(512)S(1)}, f32[512]{0:T(512)S(1)}, f32[512]{0:T(512)S(1)}, f32[512]{0:T(512)S(1)}, /*index=5*/f32[512]{0:T(51...) fusion(f32[1,38,14,512]{3,2,1,0:T(8,128)S(1)} %get-tuple-elemen, ...), kind=kLoop, calls=%fused_computation.181 | loop fusion | flops 4318720 | bytes 8421376 | tf_op jit(solution)/shard_map/transpose(jvp())/reduce_sum | solution.py:124
  52.4 0.9 fusion.87
  53.3 1.0 fusion.88
  55.9 0.6 fusion
  56.9 1.7 %constant_dynamic-slice_fusion = bf16[2176,512]{1,0:T(8,128)(2,1)} fusion(bf16[4352,512]{1,0:T(8,128)(2,1)S(1)} %bitcast.310, s32[]{:T(128)S(6)} %select_n.124), kind=kLoop, calls=%fused_computation.296 | loop fusion | bytes 4456452 | tf_op jit(solution)/shard_map/dynamic_slice | solution.py:40
  58.6 1.1 copy-done
  61.5 0.9 bitcast_multiply_fusion.46
  62.4 1.3 bitcast_multiply_fusion.47
  63.8 1.3 bitcast_multiply_fusion.48
  65.1 2.3 %convert_add_fusion = bf16[2176,512]{1,0:T(8,128)(2,1)S(1)} fusion(bf16[2176,512]{1,0:T(8,128)(2,1)} %collective-permute-done.8, bf16[4352,512]{1,0:T(8,128)(2,1)S(1)} %bitcast.313, s32[]{:T(128)S(6)} %select_n.123), kind=kLoop, calls=%fused_computation.1 | loop fusion | flops 4456448 | bytes 6684676 | tf_op jit(solution)/shard_map/add | solution.py:42
  67.5 0.8 collective-permute-start.9
  68.2 6.7 %pad_add_fusion = f32[1,38,14,512]{3,2,1,0:T(8,128)S(1)} fusion(f32[1,32,8,512]{3,2,1,0:T(8,128)S(1)} %get-tuple-element.96, f32[1,32,8,512]{3,2,1,0:T(8,128)S(1)} %get-tuple-element.97, f32[1,32,8,512]{3,2,1,0:T(8,128)S(1)} %get-tuple-element.98, f32[1,32,8,512]{3,2,1,0:T(8,128)S(1)} %get-tuple-element.99, f32[1,32,8,512]{3,2,1,0:T(8,128)S(1)} %get-tuple-element.100, ...), kind=kLoop, calls=%fused_computation.31 | loop fusion | flops 13074432 | bytes 26779648 | tf_op jit(solution)/shard_map/transpose(jvp())/add_any | solution.py:124
  76.0 1.8 %collective-permute-start.6 = (bf16[1,32,3,512]{3,2,1,0:T(4,128)(2,1)S(1)}, bf16[1,32,3,512]{3,2,1,0:T(4,128)(2,1)S(1)}, u32[]{:S(2)}, u32[]{:S(2)}) collective-permute-start(bf16[1,32,3,512]{3,2,1,0:T(4,128)(2,1)S(1)} %fusion.96), channel_id=1, source_target_pairs={{0,4},{4,8},{8,12},{12,16},{16,20},{20,24},{24,28},{28,32},{32,36}... | collective-permute-start | bytes 294920 | tf_op jit(solution)/shard_map/ppermute | solution.py:20
  77.8 16.3 %collective-permute-done.9 = bf16[1088,512]{1,0:T(8,128)(2,1)S(1)} collective-permute-done((bf16[1088,512]{1,0:T(8,128)(2,1)S(1)}, bf16[1088,512]{1,0:T(8,128)(2,1)S(1)}, u32[]{:S(2)}, u32[]{:S(2)}) %collective-permute-start.9) | collective-permute-done | bytes 1114144 | tf_op jit(solution)/shard_map/ppermute | solution.py:31
  94.5 1.0 collective-permute-start.10
  95.5 1.1 collective-permute-start.12
  96.7 1.4 collective-permute-start.11
  98.1 1.4 fusion.9
  99.6 6.1 %collective-permute-done.10 = bf16[272,512]{1,0:T(8,128)(2,1)S(1)} collective-permute-done((bf16[272,512]{1,0:T(8,128)(2,1)S(1)}, bf16[272,512]{1,0:T(8,128)(2,1)S(1)}, u32[]{:S(2)}, u32[]{:S(2)}) %collective-permute-start.10) | collective-permute-done | bytes 278560 | tf_op jit(solution)/shard_map/ppermute | solution.py:85
  105.7 4.1 %collective-permute-done.12 = bf16[272,512]{1,0:T(8,128)(2,1)S(1)} collective-permute-done((bf16[272,512]{1,0:T(8,128)(2,1)S(1)}, bf16[272,512]{1,0:T(8,128)(2,1)S(1)}, u32[]{:S(2)}, u32[]{:S(2)}) %collective-permute-start.12) | collective-permute-done | bytes 278560 | tf_op jit(solution)/shard_map/ppermute | solution.py:85
  110.1 3.4 %collective-permute-start.13 = (bf16[68,512]{1,0:T(8,128)(2,1)S(1)}, bf16[68,512]{1,0:T(8,128)(2,1)S(1)}, u32[]{:S(2)}, u32[]{:S(2)}) collective-permute-start(bf16[68,512]{1,0:T(8,128)(2,1)S(1)} %get-tuple-element.92), channel_id=1, source_target_pairs={{0,32},{4,36},{8,40},{12,44},{16,48},{20,52},{24,56},{28,60},{32,0... | collective-permute-start | bytes 208904 | tf_op jit(solution)/shard_map/ppermute | solution.py:85
  113.4 6.9 %collective-permute-start.15 = (bf16[68,512]{1,0:T(8,128)(2,1)S(1)}, bf16[68,512]{1,0:T(8,128)(2,1)S(1)}, u32[]{:S(2)}, u32[]{:S(2)}) collective-permute-start(bf16[68,512]{1,0:T(8,128)(2,1)S(1)} %get-tuple-element.93), channel_id=1, source_target_pairs={{0,48},{4,52},{8,56},{12,60},{16,32},{20,36},{24,40},{28,44},{32,1... | collective-permute-start | bytes 208904 | tf_op jit(solution)/shard_map/ppermute | solution.py:85
  120.5 5.0 %collective-permute-done.15 = bf16[68,512]{1,0:T(8,128)(2,1)S(1)} collective-permute-done((bf16[68,512]{1,0:T(8,128)(2,1)S(1)}, bf16[68,512]{1,0:T(8,128)(2,1)S(1)}, u32[]{:S(2)}, u32[]{:S(2)}) %collective-permute-start.15) | collective-permute-done | bytes 69664 | tf_op jit(solution)/shard_map/ppermute | solution.py:85
  125.5 3.8 %collective-permute-start.18 = (bf16[68,512]{1,0:T(8,128)(2,1)S(1)}, bf16[68,512]{1,0:T(8,128)(2,1)S(1)}, u32[]{:S(2)}, u32[]{:S(2)}) collective-permute-start(bf16[68,512]{1,0:T(8,128)(2,1)S(1)} %add_convert_fusion.1), channel_id=1, source_target_pairs={{0,192},{4,196},{8,200},{12,204},{16,208},{20,212},{24,216},{28,22... | collective-permute-start | bytes 208904 | tf_op jit(solution)/shard_map/ppermute | solution.py:85
  129.4 4.2 %collective-permute-start.17 = (bf16[68,512]{1,0:T(8,128)(2,1)S(1)}, bf16[68,512]{1,0:T(8,128)(2,1)S(1)}, u32[]{:S(2)}, u32[]{:S(2)}) collective-permute-start(bf16[68,512]{1,0:T(8,128)(2,1)S(1)} %add_convert_fusion.1), channel_id=1, source_target_pairs={{0,64},{4,68},{8,72},{12,76},{16,80},{20,84},{24,88},{28,92},{32,9... | collective-permute-start | bytes 208904 | tf_op jit(solution)/shard_map/ppermute | solution.py:85
  133.6 1.2 collective-permute-start.16
  134.9 4.4 %collective-permute-done.18 = bf16[68,512]{1,0:T(8,128)(2,1)S(1)} collective-permute-done((bf16[68,512]{1,0:T(8,128)(2,1)S(1)}, bf16[68,512]{1,0:T(8,128)(2,1)S(1)}, u32[]{:S(2)}, u32[]{:S(2)}) %collective-permute-start.18) | collective-permute-done | bytes 69664 | tf_op jit(solution)/shard_map/ppermute | solution.py:85
  139.6 0.7 collective-permute-start.21
  140.4 1.5 collective-permute-start.20
  141.9 2.3 %collective-permute-start.19 = (bf16[68,512]{1,0:T(8,128)(2,1)S(1)}, bf16[68,512]{1,0:T(8,128)(2,1)S(1)}, u32[]{:S(2)}, u32[]{:S(2)}) collective-permute-start(bf16[68,512]{1,0:T(8,128)(2,1)S(1)} %fusion.108), channel_id=1, source_target_pairs={{0,32},{4,36},{8,40},{12,44},{16,48},{20,52},{24,56},{28,60},{32,0... | collective-permute-start | bytes 208904 | tf_op jit(solution)/shard_map/ppermute | solution.py:85
  144.3 0.7 dynamic_update_slice.24
  145.0 4.3 %collective-permute-done.19 = bf16[68,512]{1,0:T(8,128)(2,1)S(1)} collective-permute-done((bf16[68,512]{1,0:T(8,128)(2,1)S(1)}, bf16[68,512]{1,0:T(8,128)(2,1)S(1)}, u32[]{:S(2)}, u32[]{:S(2)}) %collective-permute-start.19) | collective-permute-done | bytes 69664 | tf_op jit(solution)/shard_map/ppermute | solution.py:85
  149.7 0.7 dynamic_update_slice.26
  150.5 0.7 dynamic_update_slice.27
  151.6 1.1 collective-permute-start.23
  152.7 0.9 pad_maximum_fusion.11
  153.6 3.1 %collective-permute-start.24 = (bf16[272,512]{1,0:T(8,128)(2,1)S(1)}, bf16[272,512]{1,0:T(8,128)(2,1)S(1)}, u32[]{:S(2)}, u32[]{:S(2)}) collective-permute-start(bf16[272,512]{1,0:T(8,128)(2,1)S(1)} %dynamic_update_slice.27), channel_id=1, source_target_pairs={{0,12},{4,8},{8,4},{12,0},{16,28},{20,24},{24,20},{28,16},{32,44},... | collective-permute-start | bytes 835592 | tf_op jit(solution)/shard_map/ppermute | solution.py:85
  156.8 5.5 %collective-permute-done.22 = bf16[272,512]{1,0:T(8,128)(2,1)S(1)} collective-permute-done((bf16[272,512]{1,0:T(8,128)(2,1)S(1)}, bf16[272,512]{1,0:T(8,128)(2,1)S(1)}, u32[]{:S(2)}, u32[]{:S(2)}) %collective-permute-start.22) | collective-permute-done | bytes 278560 | tf_op jit(solution)/shard_map/ppermute | solution.py:85
  162.9 3.0 %collective-permute-done.24 = bf16[272,512]{1,0:T(8,128)(2,1)S(1)} collective-permute-done((bf16[272,512]{1,0:T(8,128)(2,1)S(1)}, bf16[272,512]{1,0:T(8,128)(2,1)S(1)}, u32[]{:S(2)}, u32[]{:S(2)}) %collective-permute-start.24) | collective-permute-done | bytes 278560 | tf_op jit(solution)/shard_map/ppermute | solution.py:85
  166.0 0.6 slice.891
  166.6 0.7 slice.890
  167.2 1.6 fusion.121
  (99 shorter events, 10.2 us)
Async XLA Ops:
  0.6 14.4 %copy-start.2 = (bf16[1,32,8,512]{3,2,1,0:T(8,128)(2,1)S(1)}, bf16[1,32,8,512]{3,2,1,0:T(8,128)(2,1)}, u32[]{:S(2)}) copy-start(bf16[1,32,8,512]{3,2,1,0:T(8,128)(2,1)} %param.7) | copy-start | bytes 786436
  1.8 12.9 %collective-permute-start.1 = (bf16[1,32,3,512]{3,2,1,0:T(4,128)(2,1)S(1)}, bf16[1,32,3,512]{3,2,1,0:T(4,128)(2,1)S(1)}, u32[]{:S(2)}, u32[]{:S(2)}) collective-permute-start(bf16[1,32,3,512]{3,2,1,0:T(4,128)(2,1)S(1)} %get-tuple-element.144), channel_id=1, source_target_pairs={{0,4},{4,8},{8,12},{12,16},{16,20},{20,24},{24,28},{28,32},{32,36}... | collective-permute-start | bytes 294920 | tf_op jit(solution)/shard_map/ppermute | solution.py:20
  3.4 11.5 %collective-permute-start.2 = (bf16[1,32,3,512]{3,2,1,0:T(4,128)(2,1)S(1)}, bf16[1,32,3,512]{3,2,1,0:T(4,128)(2,1)S(1)}, u32[]{:S(2)}, u32[]{:S(2)}) collective-permute-start(bf16[1,32,3,512]{3,2,1,0:T(4,128)(2,1)S(1)} %get-tuple-element.145), channel_id=1, source_target_pairs={{4,0},{8,4},{12,8},{16,12},{20,16},{24,20},{28,24},{32,28},{36,32}... | collective-permute-start | bytes 294920 | tf_op jit(solution)/shard_map/ppermute | solution.py:22
  6.1 14.3 %collective-permute-start = (bf16[512,512]{1,0:T(8,128)(2,1)}, bf16[512,512]{1,0:T(8,128)(2,1)}, u32[]{:S(2)}, u32[]{:S(2)}) collective-permute-start(bf16[512,512]{1,0:T(8,128)(2,1)} %param.11), channel_id=1, source_target_pairs={{0,2},{1,3},{2,0},{3,1},{4,6},{5,7},{6,4},{7,5},{8,10},{9,11},{10,... | collective-permute-start | bytes 1572872 | tf_op jit(solution)/shard_map/ppermute | solution.py:31
  15.4 4.8 %copy-start.9 = (f32[512]{0:T(512)S(1)}, f32[512]{0:T(512)}, u32[]{:S(2)}) copy-start(f32[512]{0:T(512)} %param.10) | copy-start | bytes 6148
  22.7 3.0 %collective-permute-start.3 = (bf16[2,512,512]{2,1,0:T(8,128)(2,1)}, bf16[2,512,512]{2,1,0:T(8,128)(2,1)}, u32[]{:S(2)}, u32[]{:S(2)}) collective-permute-start(bf16[2,512,512]{2,1,0:T(8,128)(2,1)} %pad_maximum_fusion.4), channel_id=1, source_target_pairs={{0,1},{1,0},{2,3},{3,2},{4,5},{5,4},{6,7},{7,6},{8,9},{9,8},{10,11... | collective-permute-start | bytes 3145736 | tf_op jit(solution)/shard_map/ppermute | solution.py:31
  27.4 1.5 copy-start.7
  28.9 14.1 %collective-permute-start.4 = (bf16[512,512]{1,0:T(8,128)(2,1)S(1)}, bf16[512,512]{1,0:T(8,128)(2,1)}, u32[]{:S(2)}, u32[]{:S(2)}) collective-permute-start(bf16[512,512]{1,0:T(8,128)(2,1)S(1)} %copy-done.7), channel_id=1, source_target_pairs={{0,2},{1,3},{2,0},{3,1},{4,6},{5,7},{6,4},{7,5},{8,10},{9,11},{10,... | collective-permute-start | bytes 1572872 | tf_op jit(solution)/shard_map/ppermute | solution.py:31
  29.7 13.3 %copy-start.8 = (bf16[512,512]{1,0:T(8,128)(2,1)S(1)}, bf16[512,512]{1,0:T(8,128)(2,1)}, u32[]{:S(2)}) copy-start(bf16[512,512]{1,0:T(8,128)(2,1)} %param.12) | copy-start | bytes 1572868
  44.2 3.2 %collective-permute-start.5 = (bf16[2,512,512]{2,1,0:T(8,128)(2,1)S(1)}, bf16[2,512,512]{2,1,0:T(8,128)(2,1)S(1)}, u32[]{:S(2)}, u32[]{:S(2)}) collective-permute-start(bf16[2,512,512]{2,1,0:T(8,128)(2,1)S(1)} %pad_maximum_fusion.5), channel_id=1, source_target_pairs={{0,1},{1,0},{2,3},{3,2},{4,5},{5,4},{6,7},{7,6},{8,9},{9,8},{10,11... | collective-permute-start | bytes 3145736 | tf_op jit(solution)/shard_map/ppermute | solution.py:31
  44.5 1.0 copy-start.1
  45.3 1.2 copy-start.5
  47.9 1.4 copy-start.3
  56.9 2.8 %copy-start = (bf16[2,2,1088,512]{3,2,1,0:T(8,128)(2,1)}, bf16[2,2,1088,512]{3,2,1,0:T(8,128)(2,1)S(1)}, u32[]{:S(2)}) copy-start(bf16[2,2,1088,512]{3,2,1,0:T(8,128)(2,1)S(1)} %pad_maximum_fusion) | copy-start | bytes 13369348
  59.7 5.4 %collective-permute-start.8 = (bf16[2176,512]{1,0:T(8,128)(2,1)}, bf16[2176,512]{1,0:T(8,128)(2,1)}, u32[]{:S(2)}, u32[]{:S(2)}) collective-permute-start(bf16[2176,512]{1,0:T(8,128)(2,1)} %constant_dynamic-slice_fusion), channel_id=1, source_target_pairs={{0,1},{1,0},{2,3},{3,2},{4,5},{5,4},{6,7},{7,6},{8,9},{9,8},{10,11... | collective-permute-start | bytes 6684680 | tf_op jit(solution)/shard_map/ppermute | solution.py:31
  62.4 2.7 %slice-start = ((s8[4456448]{0:T(1024)(128)(4,1)}), s8[4194304]{0:T(1024)(128)(4,1)S(1)}, s32[]{:S(2)}) async-start(s8[4456448]{0:T(1024)(128)(4,1)} %bitcast.311), calls=%async_computation | async-start | bytes 8388608
  63.8 1.4 slice-start.1
  67.5 26.6 %collective-permute-start.9 = (bf16[1088,512]{1,0:T(8,128)(2,1)S(1)}, bf16[1088,512]{1,0:T(8,128)(2,1)S(1)}, u32[]{:S(2)}, u32[]{:S(2)}) collective-permute-start(bf16[1088,512]{1,0:T(8,128)(2,1)S(1)} %dynamic-slice_convert_fusion), channel_id=1, source_target_pairs={{0,2},{1,3},{2,0},{3,1},{4,6},{5,7},{6,4},{7,5},{8,10},{9,11},{10,... | collective-permute-start | bytes 3342344 | tf_op jit(solution)/shard_map/ppermute | solution.py:31
  75.5 75.8 %collective-permute-start.7 = (bf16[1,32,3,512]{3,2,1,0:T(4,128)(2,1)S(1)}, bf16[1,32,3,512]{3,2,1,0:T(4,128)(2,1)S(1)}, u32[]{:S(2)}, u32[]{:S(2)}) collective-permute-start(bf16[1,32,3,512]{3,2,1,0:T(4,128)(2,1)S(1)} %fusion.97), channel_id=1, source_target_pairs={{4,0},{8,4},{12,8},{16,12},{20,16},{24,20},{28,24},{32,28},{36,32}... | collective-permute-start | bytes 294920 | tf_op jit(solution)/shard_map/ppermute | solution.py:22
  76.0 75.3 %collective-permute-start.6 = (bf16[1,32,3,512]{3,2,1,0:T(4,128)(2,1)S(1)}, bf16[1,32,3,512]{3,2,1,0:T(4,128)(2,1)S(1)}, u32[]{:S(2)}, u32[]{:S(2)}) collective-permute-start(bf16[1,32,3,512]{3,2,1,0:T(4,128)(2,1)S(1)} %fusion.96), channel_id=1, source_target_pairs={{0,4},{4,8},{8,12},{12,16},{16,20},{20,24},{24,28},{28,32},{32,36}... | collective-permute-start | bytes 294920 | tf_op jit(solution)/shard_map/ppermute | solution.py:20
  94.0 4.1 %copy-start.4 = (bf16[2,2,512,512]{3,2,1,0:T(8,128)(2,1)S(1)}, bf16[2,2,512,512]{3,2,1,0:T(8,128)(2,1)}, u32[]{:S(2)}) copy-start(bf16[2,2,512,512]{3,2,1,0:T(8,128)(2,1)} %copy-done.3) | copy-start | bytes 6291460
  94.4 3.7 %copy-start.6 = (bf16[256,2048]{1,0:T(8,128)(2,1)S(1)}, bf16[256,2048]{1,0:T(8,128)(2,1)}, u32[]{:S(2)}) copy-start(bf16[256,2048]{1,0:T(8,128)(2,1)} %copy-done.5) | copy-start | bytes 3145732
  94.5 11.2 %collective-permute-start.10 = (bf16[272,512]{1,0:T(8,128)(2,1)S(1)}, bf16[272,512]{1,0:T(8,128)(2,1)S(1)}, u32[]{:S(2)}, u32[]{:S(2)}) collective-permute-start(bf16[272,512]{1,0:T(8,128)(2,1)S(1)} %get-tuple-element.71), channel_id=1, source_target_pairs={{0,8},{4,12},{8,0},{12,4},{16,24},{20,28},{24,16},{28,20},{32,40},... | collective-permute-start | bytes 835592 | tf_op jit(solution)/shard_map/ppermute | solution.py:85
  95.5 14.3 %collective-permute-start.12 = (bf16[272,512]{1,0:T(8,128)(2,1)S(1)}, bf16[272,512]{1,0:T(8,128)(2,1)S(1)}, u32[]{:S(2)}, u32[]{:S(2)}) collective-permute-start(bf16[272,512]{1,0:T(8,128)(2,1)S(1)} %get-tuple-element.72), channel_id=1, source_target_pairs={{0,12},{4,8},{8,4},{12,0},{16,28},{20,24},{24,20},{28,16},{32,44},... | collective-permute-start | bytes 835592 | tf_op jit(solution)/shard_map/ppermute | solution.py:85
  96.7 13.1 %collective-permute-start.11 = (bf16[272,512]{1,0:T(8,128)(2,1)S(1)}, bf16[272,512]{1,0:T(8,128)(2,1)S(1)}, u32[]{:S(2)}, u32[]{:S(2)}) collective-permute-start(bf16[272,512]{1,0:T(8,128)(2,1)S(1)} %get-tuple-element.73), channel_id=1, source_target_pairs={{0,4},{4,0},{8,12},{12,8},{16,20},{20,16},{24,28},{28,24},{32,36},... | collective-permute-start | bytes 835592 | tf_op jit(solution)/shard_map/ppermute | solution.py:85
  110.1 10.4 %collective-permute-start.13 = (bf16[68,512]{1,0:T(8,128)(2,1)S(1)}, bf16[68,512]{1,0:T(8,128)(2,1)S(1)}, u32[]{:S(2)}, u32[]{:S(2)}) collective-permute-start(bf16[68,512]{1,0:T(8,128)(2,1)S(1)} %get-tuple-element.92), channel_id=1, source_target_pairs={{0,32},{4,36},{8,40},{12,44},{16,48},{20,52},{24,56},{28,60},{32,0... | collective-permute-start | bytes 208904 | tf_op jit(solution)/shard_map/ppermute | solution.py:85
  113.4 12.1 %collective-permute-start.15 = (bf16[68,512]{1,0:T(8,128)(2,1)S(1)}, bf16[68,512]{1,0:T(8,128)(2,1)S(1)}, u32[]{:S(2)}, u32[]{:S(2)}) collective-permute-start(bf16[68,512]{1,0:T(8,128)(2,1)S(1)} %get-tuple-element.93), channel_id=1, source_target_pairs={{0,48},{4,52},{8,56},{12,60},{16,32},{20,36},{24,40},{28,44},{32,1... | collective-permute-start | bytes 208904 | tf_op jit(solution)/shard_map/ppermute | solution.py:85
  120.4 5.1 %collective-permute-start.14 = (bf16[68,512]{1,0:T(8,128)(2,1)S(1)}, bf16[68,512]{1,0:T(8,128)(2,1)S(1)}, u32[]{:S(2)}, u32[]{:S(2)}) collective-permute-start(bf16[68,512]{1,0:T(8,128)(2,1)S(1)} %get-tuple-element.94), channel_id=1, source_target_pairs={{0,16},{4,20},{8,24},{12,28},{16,0},{20,4},{24,8},{28,12},{32,48},... | collective-permute-start | bytes 208904 | tf_op jit(solution)/shard_map/ppermute | solution.py:85
  125.5 13.7 %collective-permute-start.18 = (bf16[68,512]{1,0:T(8,128)(2,1)S(1)}, bf16[68,512]{1,0:T(8,128)(2,1)S(1)}, u32[]{:S(2)}, u32[]{:S(2)}) collective-permute-start(bf16[68,512]{1,0:T(8,128)(2,1)S(1)} %add_convert_fusion.1), channel_id=1, source_target_pairs={{0,192},{4,196},{8,200},{12,204},{16,208},{20,212},{24,216},{28,22... | collective-permute-start | bytes 208904 | tf_op jit(solution)/shard_map/ppermute | solution.py:85
  129.4 10.1 %collective-permute-start.17 = (bf16[68,512]{1,0:T(8,128)(2,1)S(1)}, bf16[68,512]{1,0:T(8,128)(2,1)S(1)}, u32[]{:S(2)}, u32[]{:S(2)}) collective-permute-start(bf16[68,512]{1,0:T(8,128)(2,1)S(1)} %add_convert_fusion.1), channel_id=1, source_target_pairs={{0,64},{4,68},{8,72},{12,76},{16,80},{20,84},{24,88},{28,92},{32,9... | collective-permute-start | bytes 208904 | tf_op jit(solution)/shard_map/ppermute | solution.py:85
  133.6 5.9 %collective-permute-start.16 = (bf16[68,512]{1,0:T(8,128)(2,1)S(1)}, bf16[68,512]{1,0:T(8,128)(2,1)S(1)}, u32[]{:S(2)}, u32[]{:S(2)}) collective-permute-start(bf16[68,512]{1,0:T(8,128)(2,1)S(1)} %add_convert_fusion.1), channel_id=1, source_target_pairs={{0,128},{4,132},{8,136},{12,140},{16,144},{20,148},{24,152},{28,15... | collective-permute-start | bytes 208904 | tf_op jit(solution)/shard_map/ppermute | solution.py:85
  139.6 10.8 %collective-permute-start.21 = (bf16[68,512]{1,0:T(8,128)(2,1)S(1)}, bf16[68,512]{1,0:T(8,128)(2,1)S(1)}, u32[]{:S(2)}, u32[]{:S(2)}) collective-permute-start(bf16[68,512]{1,0:T(8,128)(2,1)S(1)} %fusion.108), channel_id=1, source_target_pairs={{0,48},{4,52},{8,56},{12,60},{16,32},{20,36},{24,40},{28,44},{32,1... | collective-permute-start | bytes 208904 | tf_op jit(solution)/shard_map/ppermute | solution.py:85
  140.4 9.3 %collective-permute-start.20 = (bf16[68,512]{1,0:T(8,128)(2,1)S(1)}, bf16[68,512]{1,0:T(8,128)(2,1)S(1)}, u32[]{:S(2)}, u32[]{:S(2)}) collective-permute-start(bf16[68,512]{1,0:T(8,128)(2,1)S(1)} %fusion.108), channel_id=1, source_target_pairs={{0,16},{4,20},{8,24},{12,28},{16,0},{20,4},{24,8},{28,12},{32,48},... | collective-permute-start | bytes 208904 | tf_op jit(solution)/shard_map/ppermute | solution.py:85
  141.9 7.4 %collective-permute-start.19 = (bf16[68,512]{1,0:T(8,128)(2,1)S(1)}, bf16[68,512]{1,0:T(8,128)(2,1)S(1)}, u32[]{:S(2)}, u32[]{:S(2)}) collective-permute-start(bf16[68,512]{1,0:T(8,128)(2,1)S(1)} %fusion.108), channel_id=1, source_target_pairs={{0,32},{4,36},{8,40},{12,44},{16,48},{20,52},{24,56},{28,60},{32,0... | collective-permute-start | bytes 208904 | tf_op jit(solution)/shard_map/ppermute | solution.py:85
  151.2 11.2 %collective-permute-start.22 = (bf16[272,512]{1,0:T(8,128)(2,1)S(1)}, bf16[272,512]{1,0:T(8,128)(2,1)S(1)}, u32[]{:S(2)}, u32[]{:S(2)}) collective-permute-start(bf16[272,512]{1,0:T(8,128)(2,1)S(1)} %dynamic_update_slice.27), channel_id=1, source_target_pairs={{0,8},{4,12},{8,0},{12,4},{16,24},{20,28},{24,16},{28,20},{32,40},... | collective-permute-start | bytes 835592 | tf_op jit(solution)/shard_map/ppermute | solution.py:85
  151.6 11.3 %collective-permute-start.23 = (bf16[272,512]{1,0:T(8,128)(2,1)S(1)}, bf16[272,512]{1,0:T(8,128)(2,1)S(1)}, u32[]{:S(2)}, u32[]{:S(2)}) collective-permute-start(bf16[272,512]{1,0:T(8,128)(2,1)S(1)} %dynamic_update_slice.27), channel_id=1, source_target_pairs={{0,4},{4,0},{8,12},{12,8},{16,20},{20,16},{24,28},{28,24},{32,36},... | collective-permute-start | bytes 835592 | tf_op jit(solution)/shard_map/ppermute | solution.py:85
  153.6 12.4 %collective-permute-start.24 = (bf16[272,512]{1,0:T(8,128)(2,1)S(1)}, bf16[272,512]{1,0:T(8,128)(2,1)S(1)}, u32[]{:S(2)}, u32[]{:S(2)}) collective-permute-start(bf16[272,512]{1,0:T(8,128)(2,1)S(1)} %dynamic_update_slice.27), channel_id=1, source_target_pairs={{0,12},{4,8},{8,4},{12,0},{16,28},{20,24},{24,20},{28,16},{32,44},... | collective-permute-start | bytes 835592 | tf_op jit(solution)/shard_map/ppermute | solution.py:85

commit v2 on v0

--- a/solution.py
+++ b/solution.py
@@ -46,7 +46,7 @@
 def tile_summed(chunk):
     assert lax.axis_size("tile") == 64
     me = lax.axis_index("tile")
-    groups = ((0, 1), (2, 3), (4, 5))
+    groups = ((2, 3), (0, 1), (4, 5))
 
     def masks(group):
         mine = ((me >> group[0]) & 1) * 2 + ((me >> group[1]) & 1)

time: 169 us -> 180 us (1.065); the launches traced: 167 us -> 180 us
  waiting for transfers between devices: 66.9 us -> 79.3 us
    ppermute x15, waiting for transfers between devices: 32.6 us -> 45 us  [swapped(): return lax.ppermute(value, axis, [(i, i ^ mask) for i in range(count)])]
  transfers between devices with their start and end apart: 23 -> 23, of which waited for: 11 -> 11; matrix products, arithmetic and copies ran while one was open for 15% -> 14% of each run, Pallas kernels for 0% -> 0%
where the time goes in v2:
time: 180 us
  waiting for transfers between devices  79.3 us (44%)
  starting transfers between devices  42.4 us (24%)
  other arithmetic  33.6 us (19%)
  local copies, waits for them, and re-layouts  12.4 us (7%)
  matrix products  6.93 us (4%)
  between operations  5.25 us (3%)
    ppermute x15, waiting for transfers between devices, swapped(): return lax.ppermute(value, axis, [(i, i ^ mask) for i in range(count)])  45 us
    ppermute x4, waiting for transfers between devices, exchange(): return lax.ppermute(value, axis, [(i, i ^ 1 << bit) for i in range(count)])  34.3 us
    ppermute x15, starting transfers between devices, swapped(): return lax.ppermute(value, axis, [(i, i ^ mask) for i in range(count)])  32.6 us
    add_any x1, other arithmetic, depthwise(): padded[:, row:row + height, col:col + width, :] * kernel[7 * row + col]  6.73 us
    reduce_sum x1, other arithmetic, body(): mean = jnp.mean(rows, axis=-1, keepdims=True)  4.43 us
    reduce_sum x3, other arithmetic, depthwise(): padded[:, row:row + height, col:col + width, :] * kernel[7 * row + col]  4.1 us
  transfers between devices with their start and end apart: 23, of which 11 were waited for; matrix products, arithmetic and copies ran while one was open for 14% of the time, Pallas kernels for 0%

profile of v2, /device:TPU:32, one launch (start us, length us, event | category | flops | bytes accessed | tf_op | source)
XLA Modules:
  0.0 179.9 jit_solution(16578366419154497333)
XLA Ops:
  0.7 1.2 fusion.122
  1.8 1.6 collective-permute-start.1
  3.4 2.6 %collective-permute-start.2 = (bf16[1,32,3,512]{3,2,1,0:T(4,128)(2,1)S(1)}, bf16[1,32,3,512]{3,2,1,0:T(4,128)(2,1)S(1)}, u32[]{:S(2)}, u32[]{:S(2)}) collective-permute-start(bf16[1,32,3,512]{3,2,1,0:T(4,128)(2,1)S(1)} %get-tuple-element.137), channel_id=1, source_target_pairs={{4,0},{8,4},{12,8},{16,12},{20,16},{24,20},{28,24},{32,28},{36,32}... | collective-permute-start | bytes 294920 | tf_op jit(solution)/shard_map/ppermute | solution.py:22
  6.1 2.3 %pad_maximum_fusion.4 = bf16[2,512,512]{2,1,0:T(8,128)(2,1)} fusion(bf16[1,512,512]{2,1,0:T(8,128)(2,1)} %bitcast.314, bf16[1,512,512]{2,1,0:T(8,128)(2,1)} %bitcast.316), kind=kLoop, calls=%fused_computation.38 | loop fusion | flops 524288 | bytes 2097152 | tf_op jit(solution)/shard_map/stack | solution.py:150
  8.3 1.6 collective-permute-start
  10.0 0.6 fusion.126
  13.8 4.4 %fusion.118 = (f32[32,8]{1,0:T(8,128)S(1)}, f32[1,32,8,512]{3,2,1,0:T(8,128)S(1)}) fusion(f32[512]{0:T(512)S(1)} %bitcast.340, bf16[1,38,14,512]{3,2,1,0:T(8,128)(2,1)S(1)} %get-tuple-element.64, f32[512]{0:T(512)S(1)} %bitcast.358, f32[512]{0:T(512)S(1)} %bitcast.394, f32[512]{0:T(512)S(1)} %bitcast.396, f32[512]{0:T(512)S(1)} %bitcast.398, ...), kind=kLoop, calls=%fused_computation.303 | loop fusion | flops 21626624 | bytes 12094464 | tf_op jit(solution)/shard_map/reduce_sum | solution.py:143
  18.8 14.2 %collective-permute-done = bf16[2,512,512]{2,1,0:T(8,128)(2,1)} collective-permute-done((bf16[2,512,512]{2,1,0:T(8,128)(2,1)}, bf16[2,512,512]{2,1,0:T(8,128)(2,1)}, u32[]{:S(2)}, u32[]{:S(2)}) %collective-permute-start) | collective-permute-done | bytes 1048608 | tf_op jit(solution)/shard_map/ppermute | solution.py:31
  33.0 1.5 select_bitcast_fusion.3
  34.5 1.5 pad_maximum_fusion.2
  36.1 4.4 %collective-permute-done.3 = bf16[2,2,512,512]{3,2,1,0:T(8,128)(2,1)} collective-permute-done((bf16[2,2,512,512]{3,2,1,0:T(8,128)(2,1)}, bf16[2,2,512,512]{3,2,1,0:T(8,128)(2,1)}, u32[]{:S(2)}, u32[]{:S(2)}) %collective-permute-start.3) | collective-permute-done | bytes 2097184 | tf_op jit(solution)/shard_map/ppermute | solution.py:31
  40.5 2.5 %select_bitcast_fusion.1 = (bf16[2,1,2,512,512]{4,3,2,1,0:T(8,128)(2,1)S(1)}, bf16[2,1,2,512,512]{4,3,2,1,0:T(8,128)(2,1)S(1)}) fusion(bf16[2,2,512,512]{3,2,1,0:T(8,128)(2,1)} %pad_maximum_fusion.2, bf16[2,2,512,512]{3,2,1,0:T(8,128)(2,1)} %collective-permute-done.3, pred[]{:T(512)S(6)} %eq.9), kind=kLoop, calls=%fused_computation.22 | loop fusion | flops 2097152 | bytes 8388609 | tf_op jit(solution)/shard_map/stack | solution.py:96
  43.0 0.4 pad_maximum_fusion.1
  43.8 0.8 multiply_convert_fusion
  44.6 0.4 copy-done.3
  44.9 1.3 fusion.3
  46.2 0.9 multiply_reduce_fusion
  47.1 2.1 %fusion.86 = (f32[512]{0:T(512)S(1)}, f32[512]{0:T(512)S(1)}, f32[512]{0:T(512)S(1)}, f32[512]{0:T(512)S(1)}, f32[512]{0:T(512)S(1)}, /*index=5*/f32[512]{0:T(51...) fusion(f32[1,38,14,512]{3,2,1,0:T(8,128)S(1)} %get-tuple-elemen, ...), kind=kLoop, calls=%fused_computation.180 | loop fusion | flops 4318720 | bytes 8421376 | tf_op jit(solution)/shard_map/transpose(jvp())/reduce_sum | solution.py:122
  49.3 0.9 fusion.87
  50.2 1.0 fusion.88
  52.5 0.3 convolution_bitcast_fusion.1
  52.8 0.3 convolution_bitcast_fusion.2
  54.2 0.6 fusion
  54.7 0.6 fusion.1
  55.4 0.3 pad_maximum_fusion
  55.7 1.7 constant_dynamic-slice_fusion
  57.4 1.1 copy-done
  60.0 0.9 bitcast_multiply_fusion.46
  60.8 1.3 bitcast_multiply_fusion.47
  62.1 1.3 bitcast_multiply_fusion.48
  63.4 2.3 %convert_add_fusion = bf16[2176,512]{1,0:T(8,128)(2,1)S(1)} fusion(bf16[2176,512]{1,0:T(8,128)(2,1)} %collective-permute-done.6, bf16[4352,512]{1,0:T(8,128)(2,1)S(1)} %bitcast.307, s32[]{:T(128)S(6)} %select_n.103), kind=kLoop, calls=%fused_computation.1 | loop fusion | flops 4456448 | bytes 6684676 | tf_op jit(solution)/shard_map/add | solution.py:42
  65.8 1.7 collective-permute-start.7
  67.4 6.7 %pad_add_fusion = f32[1,38,14,512]{3,2,1,0:T(8,128)S(1)} fusion(f32[1,32,8,512]{3,2,1,0:T(8,128)S(1)} %get-tuple-element.88, f32[1,32,8,512]{3,2,1,0:T(8,128)S(1)} %get-tuple-element.89, f32[1,32,8,512]{3,2,1,0:T(8,128)S(1)} %get-tuple-element.90, f32[1,32,8,512]{3,2,1,0:T(8,128)S(1)} %get-tuple-element.91, f32[1,32,8,512]{3,2,1,0:T(8,128)S(1)} %get-tuple-element.92, ...), kind=kLoop, calls=%fused_computation.33 | loop fusion | flops 13074432 | bytes 26779648 | tf_op jit(solution)/shard_map/transpose(jvp())/add_any | solution.py:122
  74.6 0.4 collective-permute-start.5
  75.2 1.8 %collective-permute-start.4 = (bf16[1,32,3,512]{3,2,1,0:T(4,128)(2,1)S(1)}, bf16[1,32,3,512]{3,2,1,0:T(4,128)(2,1)S(1)}, u32[]{:S(2)}, u32[]{:S(2)}) collective-permute-start(bf16[1,32,3,512]{3,2,1,0:T(4,128)(2,1)S(1)} %fusion.96), channel_id=1, source_target_pairs={{0,4},{4,8},{8,12},{12,16},{16,20},{20,24},{24,28},{28,32},{32,36}... | collective-permute-start | bytes 294920 | tf_op jit(solution)/shard_map/ppermute | solution.py:20
  77.0 15.7 %collective-permute-done.7 = bf16[1088,512]{1,0:T(8,128)(2,1)S(1)} collective-permute-done((bf16[1088,512]{1,0:T(8,128)(2,1)S(1)}, bf16[1088,512]{1,0:T(8,128)(2,1)S(1)}, u32[]{:S(2)}, u32[]{:S(2)}) %collective-permute-start.7) | collective-permute-done | bytes 1114144 | tf_op jit(solution)/shard_map/ppermute | solution.py:31
  92.7 0.3 convert_add_fusion.1
  93.2 3.4 %collective-permute-start.8 = (bf16[272,512]{1,0:T(8,128)(2,1)S(1)}, bf16[272,512]{1,0:T(8,128)(2,1)S(1)}, u32[]{:S(2)}, u32[]{:S(2)}) collective-permute-start(bf16[272,512]{1,0:T(8,128)(2,1)S(1)} %get-tuple-element.73), channel_id=1, source_target_pairs={{0,32},{4,36},{8,40},{12,44},{16,48},{20,52},{24,56},{28,60},{32,0... | collective-permute-start | bytes 835592 | tf_op jit(solution)/shard_map/ppermute | solution.py:85
  96.5 8.0 %collective-permute-start.10 = (bf16[272,512]{1,0:T(8,128)(2,1)S(1)}, bf16[272,512]{1,0:T(8,128)(2,1)S(1)}, u32[]{:S(2)}, u32[]{:S(2)}) collective-permute-start(bf16[272,512]{1,0:T(8,128)(2,1)S(1)} %get-tuple-element.74), channel_id=1, source_target_pairs={{0,48},{4,52},{8,56},{12,60},{16,32},{20,36},{24,40},{28,44},{32,1... | collective-permute-start | bytes 835592 | tf_op jit(solution)/shard_map/ppermute | solution.py:85
  104.5 1.4 fusion.9
  106.0 16.6 %collective-permute-done.10 = bf16[272,512]{1,0:T(8,128)(2,1)S(1)} collective-permute-done((bf16[272,512]{1,0:T(8,128)(2,1)S(1)}, bf16[272,512]{1,0:T(8,128)(2,1)S(1)}, u32[]{:S(2)}, u32[]{:S(2)}) %collective-permute-start.10) | collective-permute-done | bytes 278560 | tf_op jit(solution)/shard_map/ppermute | solution.py:85
  123.0 3.4 %collective-permute-start.12 = (bf16[68,512]{1,0:T(8,128)(2,1)S(1)}, bf16[68,512]{1,0:T(8,128)(2,1)S(1)}, u32[]{:S(2)}, u32[]{:S(2)}) collective-permute-start(bf16[68,512]{1,0:T(8,128)(2,1)S(1)} %get-tuple-element.86), channel_id=1, source_target_pairs={{0,4},{4,0},{8,12},{12,8},{16,20},{20,16},{24,28},{28,24},{32,36},... | collective-permute-start | bytes 208904 | tf_op jit(solution)/shard_map/ppermute | solution.py:85
  126.5 2.3 %collective-permute-done.11 = bf16[68,512]{1,0:T(8,128)(2,1)S(1)} collective-permute-done((bf16[68,512]{1,0:T(8,128)(2,1)S(1)}, bf16[68,512]{1,0:T(8,128)(2,1)S(1)}, u32[]{:S(2)}, u32[]{:S(2)}) %collective-permute-start.11) | collective-permute-done | bytes 69664 | tf_op jit(solution)/shard_map/ppermute | solution.py:85
  128.8 0.5 collective-permute-done.13
  129.4 7.5 %collective-permute-start.16 = (bf16[68,512]{1,0:T(8,128)(2,1)S(1)}, bf16[68,512]{1,0:T(8,128)(2,1)S(1)}, u32[]{:S(2)}, u32[]{:S(2)}) collective-permute-start(bf16[68,512]{1,0:T(8,128)(2,1)S(1)} %add_convert_fusion.1), channel_id=1, source_target_pairs={{0,192},{4,196},{8,200},{12,204},{16,208},{20,212},{24,216},{28,22... | collective-permute-start | bytes 208904 | tf_op jit(solution)/shard_map/ppermute | solution.py:85
  136.9 1.7 collective-permute-start.14
  138.8 2.5 %collective-permute-done.16 = bf16[68,512]{1,0:T(8,128)(2,1)S(1)} collective-permute-done((bf16[68,512]{1,0:T(8,128)(2,1)S(1)}, bf16[68,512]{1,0:T(8,128)(2,1)S(1)}, u32[]{:S(2)}, u32[]{:S(2)}) %collective-permute-start.16) | collective-permute-done | bytes 69664 | tf_op jit(solution)/shard_map/ppermute | solution.py:85
  141.3 4.2 %collective-permute-done.15 = bf16[68,512]{1,0:T(8,128)(2,1)S(1)} collective-permute-done((bf16[68,512]{1,0:T(8,128)(2,1)S(1)}, bf16[68,512]{1,0:T(8,128)(2,1)S(1)}, u32[]{:S(2)}, u32[]{:S(2)}) %collective-permute-start.15) | collective-permute-done | bytes 69664 | tf_op jit(solution)/shard_map/ppermute | solution.py:85
  145.6 1.4 collective-permute-start.19
  147.0 3.4 %collective-permute-start.17 = (bf16[68,512]{1,0:T(8,128)(2,1)S(1)}, bf16[68,512]{1,0:T(8,128)(2,1)S(1)}, u32[]{:S(2)}, u32[]{:S(2)}) collective-permute-start(bf16[68,512]{1,0:T(8,128)(2,1)S(1)} %fusion.113), channel_id=1, source_target_pairs={{0,8},{4,12},{8,0},{12,4},{16,24},{20,28},{24,16},{28,20},{32,40},... | collective-permute-start | bytes 208904 | tf_op jit(solution)/shard_map/ppermute | solution.py:85
  150.6 0.7 dynamic_update_slice.24
  151.3 2.2 %collective-permute-done.17 = bf16[68,512]{1,0:T(8,128)(2,1)S(1)} collective-permute-done((bf16[68,512]{1,0:T(8,128)(2,1)S(1)}, bf16[68,512]{1,0:T(8,128)(2,1)S(1)}, u32[]{:S(2)}, u32[]{:S(2)}) %collective-permute-start.17) | collective-permute-done | bytes 69664 | tf_op jit(solution)/shard_map/ppermute | solution.py:85
  153.5 0.6 dynamic_update_slice.25
  154.2 0.7 dynamic_update_slice.26
  154.9 0.5 dynamic_update_slice.27
  155.5 0.3 fusion.107
  155.8 1.5 collective-permute-start.21
  157.4 0.9 pad_maximum_fusion.10
  158.3 2.0 %collective-permute-start.22 = (bf16[272,512]{1,0:T(8,128)(2,1)S(1)}, bf16[272,512]{1,0:T(8,128)(2,1)S(1)}, u32[]{:S(2)}, u32[]{:S(2)}) collective-permute-start(bf16[272,512]{1,0:T(8,128)(2,1)S(1)} %dynamic_update_slice.27), channel_id=1, source_target_pairs={{0,48},{4,52},{8,56},{12,60},{16,32},{20,36},{24,40},{28,44},{32,1... | collective-permute-start | bytes 835592 | tf_op jit(solution)/shard_map/ppermute | solution.py:85
  160.4 11.0 %collective-permute-done.20 = bf16[272,512]{1,0:T(8,128)(2,1)S(1)} collective-permute-done((bf16[272,512]{1,0:T(8,128)(2,1)S(1)}, bf16[272,512]{1,0:T(8,128)(2,1)S(1)}, u32[]{:S(2)}, u32[]{:S(2)}) %collective-permute-start.20) | collective-permute-done | bytes 278560 | tf_op jit(solution)/shard_map/ppermute | solution.py:85
  171.4 5.6 %collective-permute-done.22 = bf16[272,512]{1,0:T(8,128)(2,1)S(1)} collective-permute-done((bf16[272,512]{1,0:T(8,128)(2,1)S(1)}, bf16[272,512]{1,0:T(8,128)(2,1)S(1)}, u32[]{:S(2)}, u32[]{:S(2)}) %collective-permute-start.22) | collective-permute-done | bytes 278560 | tf_op jit(solution)/shard_map/ppermute | solution.py:85
  177.0 0.6 slice.896
  177.6 0.7 slice.895
  178.3 1.6 fusion.121
  (94 shorter events, 6.1 us)
Async XLA Ops:
  0.6 12.9 %copy-start.2 = (bf16[1,32,8,512]{3,2,1,0:T(8,128)(2,1)S(1)}, bf16[1,32,8,512]{3,2,1,0:T(8,128)(2,1)}, u32[]{:S(2)}) copy-start(bf16[1,32,8,512]{3,2,1,0:T(8,128)(2,1)} %param.7) | copy-start | bytes 786436
  0.6 9.3 %copy-start.8 = (f32[49,512]{1,0:T(8,128)S(1)}, f32[49,512]{1,0:T(8,128)}, u32[]{:S(2)}) copy-start(f32[49,512]{1,0:T(8,128)} %param.9) | copy-start | bytes 301060
  0.7 9.4 %copy-start.10 = (s32[1,2]{1,0:T(1,128)S(1)}, s32[1,2]{1,0:T(1,128)}, u32[]{:S(2)}) copy-start(s32[1,2]{1,0:T(1,128)} %param.8) | copy-start | bytes 28
  1.8 11.4 %collective-permute-start.1 = (bf16[1,32,3,512]{3,2,1,0:T(4,128)(2,1)S(1)}, bf16[1,32,3,512]{3,2,1,0:T(4,128)(2,1)S(1)}, u32[]{:S(2)}, u32[]{:S(2)}) collective-permute-start(bf16[1,32,3,512]{3,2,1,0:T(4,128)(2,1)S(1)} %get-tuple-element.136), channel_id=1, source_target_pairs={{0,4},{4,8},{8,12},{12,16},{16,20},{20,24},{24,28},{28,32},{32,36}... | collective-permute-start | bytes 294920 | tf_op jit(solution)/shard_map/ppermute | solution.py:20
  3.4 9.9 %collective-permute-start.2 = (bf16[1,32,3,512]{3,2,1,0:T(4,128)(2,1)S(1)}, bf16[1,32,3,512]{3,2,1,0:T(4,128)(2,1)S(1)}, u32[]{:S(2)}, u32[]{:S(2)}) collective-permute-start(bf16[1,32,3,512]{3,2,1,0:T(4,128)(2,1)S(1)} %get-tuple-element.137), channel_id=1, source_target_pairs={{4,0},{8,4},{12,8},{16,12},{20,16},{24,20},{28,24},{32,28},{36,32}... | collective-permute-start | bytes 294920 | tf_op jit(solution)/shard_map/ppermute | solution.py:22
  8.3 24.7 %collective-permute-start = (bf16[2,512,512]{2,1,0:T(8,128)(2,1)}, bf16[2,512,512]{2,1,0:T(8,128)(2,1)}, u32[]{:S(2)}, u32[]{:S(2)}) collective-permute-start(bf16[2,512,512]{2,1,0:T(8,128)(2,1)} %pad_maximum_fusion.4), channel_id=1, source_target_pairs={{0,2},{1,3},{2,0},{3,1},{4,6},{5,7},{6,4},{7,5},{8,10},{9,11},{10,... | collective-permute-start | bytes 3145736 | tf_op jit(solution)/shard_map/ppermute | solution.py:31
  13.8 4.9 %copy-start.9 = (f32[512]{0:T(512)S(1)}, f32[512]{0:T(512)}, u32[]{:S(2)}) copy-start(f32[512]{0:T(512)} %param.10) | copy-start | bytes 6148
  13.8 19.2 %copy-start.5 = (bf16[512,512]{1,0:T(8,128)(2,1)S(1)}, bf16[512,512]{1,0:T(8,128)(2,1)}, u32[]{:S(2)}) copy-start(bf16[512,512]{1,0:T(8,128)(2,1)} %param.12) | copy-start | bytes 1572868
  36.0 4.5 %collective-permute-start.3 = (bf16[2,2,512,512]{3,2,1,0:T(8,128)(2,1)}, bf16[2,2,512,512]{3,2,1,0:T(8,128)(2,1)}, u32[]{:S(2)}, u32[]{:S(2)}) collective-permute-start(bf16[2,2,512,512]{3,2,1,0:T(8,128)(2,1)} %pad_maximum_fusion.2), channel_id=1, source_target_pairs={{0,1},{1,0},{2,3},{3,2},{4,5},{5,4},{6,7},{7,6},{8,9},{9,8},{10,11... | collective-permute-start | bytes 6291464 | tf_op jit(solution)/shard_map/ppermute | solution.py:31
  43.6 1.4 copy-start.3
  43.8 1.2 copy-start.1
  44.5 9.0 %copy-start.6 = (bf16[256,2048]{1,0:T(8,128)(2,1)}, bf16[256,2048]{1,0:T(8,128)(2,1)S(1)}, u32[]{:S(2)}) copy-start(bf16[256,2048]{1,0:T(8,128)(2,1)S(1)} %get-tuple-element.189) | copy-start | bytes 3145732
  55.7 2.8 %copy-start = (bf16[2,2,1088,512]{3,2,1,0:T(8,128)(2,1)}, bf16[2,2,1088,512]{3,2,1,0:T(8,128)(2,1)S(1)}, u32[]{:S(2)}) copy-start(bf16[2,2,1088,512]{3,2,1,0:T(8,128)(2,1)S(1)} %pad_maximum_fusion) | copy-start | bytes 13369348
  58.5 4.9 %collective-permute-start.6 = (bf16[2176,512]{1,0:T(8,128)(2,1)}, bf16[2176,512]{1,0:T(8,128)(2,1)}, u32[]{:S(2)}, u32[]{:S(2)}) collective-permute-start(bf16[2176,512]{1,0:T(8,128)(2,1)} %constant_dynamic-slice_fusion), channel_id=1, source_target_pairs={{0,1},{1,0},{2,3},{3,2},{4,5},{5,4},{6,7},{7,6},{8,9},{9,8},{10,11... | collective-permute-start | bytes 6684680 | tf_op jit(solution)/shard_map/ppermute | solution.py:31
  60.8 2.6 %slice-start = ((s8[4456448]{0:T(1024)(128)(4,1)}), s8[4194304]{0:T(1024)(128)(4,1)S(1)}, s32[]{:S(2)}) async-start(s8[4456448]{0:T(1024)(128)(4,1)} %bitcast.305), calls=%async_computation | async-start | bytes 8388608
  62.1 1.3 slice-start.1
  65.8 26.9 %collective-permute-start.7 = (bf16[1088,512]{1,0:T(8,128)(2,1)S(1)}, bf16[1088,512]{1,0:T(8,128)(2,1)S(1)}, u32[]{:S(2)}, u32[]{:S(2)}) collective-permute-start(bf16[1088,512]{1,0:T(8,128)(2,1)S(1)} %dynamic-slice_convert_fusion), channel_id=1, source_target_pairs={{0,2},{1,3},{2,0},{3,1},{4,6},{5,7},{6,4},{7,5},{8,10},{9,11},{10,... | collective-permute-start | bytes 3342344 | tf_op jit(solution)/shard_map/ppermute | solution.py:31
  74.6 80.8 %collective-permute-start.5 = (bf16[1,32,3,512]{3,2,1,0:T(4,128)(2,1)S(1)}, bf16[1,32,3,512]{3,2,1,0:T(4,128)(2,1)S(1)}, u32[]{:S(2)}, u32[]{:S(2)}) collective-permute-start(bf16[1,32,3,512]{3,2,1,0:T(4,128)(2,1)S(1)} %fusion.97), channel_id=1, source_target_pairs={{4,0},{8,4},{12,8},{16,12},{20,16},{24,20},{28,24},{32,28},{36,32}... | collective-permute-start | bytes 294920 | tf_op jit(solution)/shard_map/ppermute | solution.py:22
  75.1 29.4 %copy-start.4 = (bf16[4,1,512,512]{3,2,1,0:T(8,128)(2,1)S(1)}, bf16[4,1,512,512]{3,2,1,0:T(8,128)(2,1)}, u32[]{:S(2)}) copy-start(bf16[4,1,512,512]{3,2,1,0:T(8,128)(2,1)} %copy-done.3) | copy-start | bytes 6291460
  75.1 29.4 %copy-start.7 = (bf16[256,2048]{1,0:T(8,128)(2,1)S(1)}, bf16[256,2048]{1,0:T(8,128)(2,1)}, u32[]{:S(2)}) copy-start(bf16[256,2048]{1,0:T(8,128)(2,1)} %copy-done.6) | copy-start | bytes 3145732
  75.2 80.3 %collective-permute-start.4 = (bf16[1,32,3,512]{3,2,1,0:T(4,128)(2,1)S(1)}, bf16[1,32,3,512]{3,2,1,0:T(4,128)(2,1)S(1)}, u32[]{:S(2)}, u32[]{:S(2)}) collective-permute-start(bf16[1,32,3,512]{3,2,1,0:T(4,128)(2,1)S(1)} %fusion.96), channel_id=1, source_target_pairs={{0,4},{4,8},{8,12},{12,16},{16,20},{20,24},{24,28},{28,32},{32,36}... | collective-permute-start | bytes 294920 | tf_op jit(solution)/shard_map/ppermute | solution.py:20
  93.2 12.8 %collective-permute-start.8 = (bf16[272,512]{1,0:T(8,128)(2,1)S(1)}, bf16[272,512]{1,0:T(8,128)(2,1)S(1)}, u32[]{:S(2)}, u32[]{:S(2)}) collective-permute-start(bf16[272,512]{1,0:T(8,128)(2,1)S(1)} %get-tuple-element.73), channel_id=1, source_target_pairs={{0,32},{4,36},{8,40},{12,44},{16,48},{20,52},{24,56},{28,60},{32,0... | collective-permute-start | bytes 835592 | tf_op jit(solution)/shard_map/ppermute | solution.py:85
  96.5 26.1 %collective-permute-start.10 = (bf16[272,512]{1,0:T(8,128)(2,1)S(1)}, bf16[272,512]{1,0:T(8,128)(2,1)S(1)}, u32[]{:S(2)}, u32[]{:S(2)}) collective-permute-start(bf16[272,512]{1,0:T(8,128)(2,1)S(1)} %get-tuple-element.74), channel_id=1, source_target_pairs={{0,48},{4,52},{8,56},{12,60},{16,32},{20,36},{24,40},{28,44},{32,1... | collective-permute-start | bytes 835592 | tf_op jit(solution)/shard_map/ppermute | solution.py:85
  104.5 18.0 %collective-permute-start.9 = (bf16[272,512]{1,0:T(8,128)(2,1)S(1)}, bf16[272,512]{1,0:T(8,128)(2,1)S(1)}, u32[]{:S(2)}, u32[]{:S(2)}) collective-permute-start(bf16[272,512]{1,0:T(8,128)(2,1)S(1)} %get-tuple-element.75), channel_id=1, source_target_pairs={{0,16},{4,20},{8,24},{12,28},{16,0},{20,4},{24,8},{28,12},{32,48},... | collective-permute-start | bytes 835592 | tf_op jit(solution)/shard_map/ppermute | solution.py:85
  122.8 6.0 %collective-permute-start.11 = (bf16[68,512]{1,0:T(8,128)(2,1)S(1)}, bf16[68,512]{1,0:T(8,128)(2,1)S(1)}, u32[]{:S(2)}, u32[]{:S(2)}) collective-permute-start(bf16[68,512]{1,0:T(8,128)(2,1)S(1)} %get-tuple-element.84), channel_id=1, source_target_pairs={{0,8},{4,12},{8,0},{12,4},{16,24},{20,28},{24,16},{28,20},{32,40},... | collective-permute-start | bytes 208904 | tf_op jit(solution)/shard_map/ppermute | solution.py:85
  122.9 6.4 %collective-permute-start.13 = (bf16[68,512]{1,0:T(8,128)(2,1)S(1)}, bf16[68,512]{1,0:T(8,128)(2,1)S(1)}, u32[]{:S(2)}, u32[]{:S(2)}) collective-permute-start(bf16[68,512]{1,0:T(8,128)(2,1)S(1)} %get-tuple-element.85), channel_id=1, source_target_pairs={{0,12},{4,8},{8,4},{12,0},{16,28},{20,24},{24,20},{28,16},{32,44},... | collective-permute-start | bytes 208904 | tf_op jit(solution)/shard_map/ppermute | solution.py:85
  123.0 6.3 %collective-permute-start.12 = (bf16[68,512]{1,0:T(8,128)(2,1)S(1)}, bf16[68,512]{1,0:T(8,128)(2,1)S(1)}, u32[]{:S(2)}, u32[]{:S(2)}) collective-permute-start(bf16[68,512]{1,0:T(8,128)(2,1)S(1)} %get-tuple-element.86), channel_id=1, source_target_pairs={{0,4},{4,0},{8,12},{12,8},{16,20},{20,16},{24,28},{28,24},{32,36},... | collective-permute-start | bytes 208904 | tf_op jit(solution)/shard_map/ppermute | solution.py:85
  129.4 11.9 %collective-permute-start.16 = (bf16[68,512]{1,0:T(8,128)(2,1)S(1)}, bf16[68,512]{1,0:T(8,128)(2,1)S(1)}, u32[]{:S(2)}, u32[]{:S(2)}) collective-permute-start(bf16[68,512]{1,0:T(8,128)(2,1)S(1)} %add_convert_fusion.1), channel_id=1, source_target_pairs={{0,192},{4,196},{8,200},{12,204},{16,208},{20,212},{24,216},{28,22... | collective-permute-start | bytes 208904 | tf_op jit(solution)/shard_map/ppermute | solution.py:85
  136.9 8.6 %collective-permute-start.15 = (bf16[68,512]{1,0:T(8,128)(2,1)S(1)}, bf16[68,512]{1,0:T(8,128)(2,1)S(1)}, u32[]{:S(2)}, u32[]{:S(2)}) collective-permute-start(bf16[68,512]{1,0:T(8,128)(2,1)S(1)} %add_convert_fusion.1), channel_id=1, source_target_pairs={{0,64},{4,68},{8,72},{12,76},{16,80},{20,84},{24,88},{28,92},{32,9... | collective-permute-start | bytes 208904 | tf_op jit(solution)/shard_map/ppermute | solution.py:85
  136.9 8.6 %collective-permute-start.14 = (bf16[68,512]{1,0:T(8,128)(2,1)S(1)}, bf16[68,512]{1,0:T(8,128)(2,1)S(1)}, u32[]{:S(2)}, u32[]{:S(2)}) collective-permute-start(bf16[68,512]{1,0:T(8,128)(2,1)S(1)} %add_convert_fusion.1), channel_id=1, source_target_pairs={{0,128},{4,132},{8,136},{12,140},{16,144},{20,148},{24,152},{28,15... | collective-permute-start | bytes 208904 | tf_op jit(solution)/shard_map/ppermute | solution.py:85
  145.6 9.3 %collective-permute-start.19 = (bf16[68,512]{1,0:T(8,128)(2,1)S(1)}, bf16[68,512]{1,0:T(8,128)(2,1)S(1)}, u32[]{:S(2)}, u32[]{:S(2)}) collective-permute-start(bf16[68,512]{1,0:T(8,128)(2,1)S(1)} %fusion.113), channel_id=1, source_target_pairs={{0,12},{4,8},{8,4},{12,0},{16,28},{20,24},{24,20},{28,16},{32,44},... | collective-permute-start | bytes 208904 | tf_op jit(solution)/shard_map/ppermute | solution.py:85
  147.0 7.2 %collective-permute-start.18 = (bf16[68,512]{1,0:T(8,128)(2,1)S(1)}, bf16[68,512]{1,0:T(8,128)(2,1)S(1)}, u32[]{:S(2)}, u32[]{:S(2)}) collective-permute-start(bf16[68,512]{1,0:T(8,128)(2,1)S(1)} %fusion.113), channel_id=1, source_target_pairs={{0,4},{4,0},{8,12},{12,8},{16,20},{20,16},{24,28},{28,24},{32,36},... | collective-permute-start | bytes 208904 | tf_op jit(solution)/shard_map/ppermute | solution.py:85
  147.0 6.5 %collective-permute-start.17 = (bf16[68,512]{1,0:T(8,128)(2,1)S(1)}, bf16[68,512]{1,0:T(8,128)(2,1)S(1)}, u32[]{:S(2)}, u32[]{:S(2)}) collective-permute-start(bf16[68,512]{1,0:T(8,128)(2,1)S(1)} %fusion.113), channel_id=1, source_target_pairs={{0,8},{4,12},{8,0},{12,4},{16,24},{20,28},{24,16},{28,20},{32,40},... | collective-permute-start | bytes 208904 | tf_op jit(solution)/shard_map/ppermute | solution.py:85
  155.4 16.0 %collective-permute-start.20 = (bf16[272,512]{1,0:T(8,128)(2,1)S(1)}, bf16[272,512]{1,0:T(8,128)(2,1)S(1)}, u32[]{:S(2)}, u32[]{:S(2)}) collective-permute-start(bf16[272,512]{1,0:T(8,128)(2,1)S(1)} %dynamic_update_slice.27), channel_id=1, source_target_pairs={{0,32},{4,36},{8,40},{12,44},{16,48},{20,52},{24,56},{28,60},{32,0... | collective-permute-start | bytes 835592 | tf_op jit(solution)/shard_map/ppermute | solution.py:85
  155.8 15.6 %collective-permute-start.21 = (bf16[272,512]{1,0:T(8,128)(2,1)S(1)}, bf16[272,512]{1,0:T(8,128)(2,1)S(1)}, u32[]{:S(2)}, u32[]{:S(2)}) collective-permute-start(bf16[272,512]{1,0:T(8,128)(2,1)S(1)} %dynamic_update_slice.27), channel_id=1, source_target_pairs={{0,16},{4,20},{8,24},{12,28},{16,0},{20,4},{24,8},{28,12},{32,48},... | collective-permute-start | bytes 835592 | tf_op jit(solution)/shard_map/ppermute | solution.py:85
  158.3 18.7 %collective-permute-start.22 = (bf16[272,512]{1,0:T(8,128)(2,1)S(1)}, bf16[272,512]{1,0:T(8,128)(2,1)S(1)}, u32[]{:S(2)}, u32[]{:S(2)}) collective-permute-start(bf16[272,512]{1,0:T(8,128)(2,1)S(1)} %dynamic_update_slice.27), channel_id=1, source_target_pairs={{0,48},{4,52},{8,56},{12,60},{16,32},{20,36},{24,40},{28,44},{32,1... | collective-permute-start | bytes 835592 | tf_op jit(solution)/shard_map/ppermute | solution.py:85
